TPU v7x, 512 devices: a whole 4x8x8 slice. The times are simulated.
512 devices in a mesh: box: 128 (over x, y_lo, z), exc: 4 (over y_hi, core).
Axes of the slice: x: 4, y: 8 (y_hi: 2, y_lo: 4; y = y_hi * 4 + y_lo), z: 8, core: 2. Of those that a mesh axis runs over, the one named last changes fastest.
Arguments:
- incident: bfloat16 [2, 8, 512, 512], P(None, 'exc', 'box'), may hold values from -7 to 7
- contrast: int32 [512, 512], P('box'), may hold values from 1 to 16
- box_pos: int32 [512], replicated, may hold values from 0 to 3, as said below
- directions: float32 [3, 512], P(None, 'box'), may hold values from -1 to 1, as said below
- enc_table: bfloat16 [2, 512, 512], replicated, may hold values from -0.25 to 0.25
- dec_table: bfloat16 [2, 512, 512], replicated, may hold values from -0.25 to 0.25
Outputs:
- scattered_one: bfloat16 [2, 8, 512, 512], P(None, 'exc', 'box')
- scattered_two: bfloat16 [2, 8, 512, 512], P(None, 'exc', 'box')
- series_ratio: float32 [512], P('box')
Inputs may be any that keep to these rules, and one draw needn't show every extreme that they name: `box_pos`: entries 4 m to 4 m + 3 hold each number from 0 to 3 once. `directions`: each column is a unit vector.
All inputs are finite; a program needn't handle non-finite values.
Results may differ from a plain program's by a relative error of at most 0.0053.
Values may be sent and summed in bfloat16 or wider, within the bound.
No kernel may reach another device: no remote copies, remote signals or barrier semaphores. Data moves between devices by JAX's collectives and lax.ppermute only.
A program may use at most 128 MiB of HBM per device.

v0:
```python
import numpy as np
import jax
import jax.numpy as jnp
from jax import lax
from jax.sharding import PartitionSpec as P

BSIDE = 8
CY = 2
CZ = 2
V = 512


wave_number = 0.8
near_scale = 0.1
self_value = 1.0
far_scale = 0.25
chi_step = 0.0625
epsilon = 1e-06


def padded(block, sides, width):
    for axis, dim in sides:
        count = lax.axis_size(axis)
        forward = [(i, i + 1) for i in range(count - 1)]
        backward = [(target, source) for source, target in forward]
        low = lax.ppermute(
            lax.slice_in_dim(block, block.shape[dim] - width, None, axis=dim), axis, forward
        )
        high = lax.ppermute(lax.slice_in_dim(block, 0, width, axis=dim), axis, backward)
        block = jnp.concatenate([low, block, high], axis=dim)
    return block


def box_coords(box_pos):
    box_count = box_pos.shape[0]
    slab_coord = (jnp.arange(box_count, dtype=jnp.int32) // (CY * CZ)).astype(jnp.float32)
    row_coord = (box_pos // CZ).astype(jnp.float32)
    col_coord = (box_pos % CZ).astype(jnp.float32)
    return (slab_coord, row_coord, col_coord)


def translator(column, coords):
    slab_gap = coords[0][:, None] - coords[0][None, :]
    row_gap = coords[1][:, None] - coords[1][None, :]
    col_gap = coords[2][:, None] - coords[2][None, :]
    square = slab_gap * slab_gap + row_gap * row_gap + col_gap * col_gap
    nearby = jnp.maximum(jnp.maximum(jnp.abs(slab_gap), jnp.abs(row_gap)), jnp.abs(col_gap)) < 1.5
    radius = jnp.sqrt(jnp.maximum(square, 1.0))
    kappa = wave_number * BSIDE
    argument = kappa * radius
    inverse = 1.0 / argument
    cosine = (column[0] * slab_gap + column[1] * row_gap + column[2] * col_gap) / radius
    prev_re, prev_im = (inverse, jnp.zeros_like(inverse))
    now_re, now_im = (jnp.zeros_like(inverse), -inverse)
    leg_prev, leg_now = (jnp.ones_like(inverse), jnp.ones_like(inverse))
    total_re = jnp.zeros_like(inverse)
    total_im = jnp.zeros_like(inverse)
    for order in range(4):
        if order == 0:
            legendre = jnp.ones_like(inverse)
        elif order == 1:
            legendre = cosine
        else:
            legendre = ((2 * order - 1) * cosine * leg_now - (order - 1) * leg_prev) / order
        leg_prev, leg_now = (leg_now, legendre)
        weight = (2.0 * order + 1.0) * legendre
        rot = order % 4
        if rot == 0:
            term_re, term_im = (now_re, now_im)
        elif rot == 1:
            term_re, term_im = (-now_im, now_re)
        elif rot == 2:
            term_re, term_im = (-now_re, -now_im)
        else:
            term_re, term_im = (now_im, -now_re)
        total_re = total_re + weight * term_re
        total_im = total_im + weight * term_im
        next_re = (2.0 * order + 1.0) * inverse * now_re - prev_re
        next_im = (2.0 * order + 1.0) * inverse * now_im - prev_im
        prev_re, prev_im = (now_re, now_im)
        now_re, now_im = (next_re, next_im)
    wave_re = jnp.cos(argument)
    wave_im = jnp.sin(argument)
    factor = jnp.where(nearby, 0.0, far_scale * kappa / 16.0)
    real_part = factor * (total_re * wave_re - total_im * wave_im)
    imag_part = factor * (total_re * wave_im + total_im * wave_re)
    return jnp.stack([real_part, imag_part]).astype(jnp.bfloat16)


def build_translators(dir_block, box_pos):
    coords = box_coords(box_pos)

    def one_direction(column):
        return translator(column, coords)

    return jax.vmap(one_direction)(jnp.transpose(dir_block))


def green_constants():
    index = np.arange(V)
    coords = np.stack([index // (BSIDE * BSIDE), index // BSIDE % BSIDE, index % BSIDE])
    blocks = []
    for base in range(8):
        offset = (base // 4, base // 2 % 2, base % 2)
        square = np.zeros((V, V), np.float64)
        for dimension in range(3):
            differ = coords[dimension][:, None] - coords[dimension][None, :] - BSIDE * offset[dimension]
            square = square + differ * differ
        radius = np.sqrt(np.maximum(square, 1.0))
        inside = square < 0.5
        real_part = np.where(inside, self_value, near_scale * np.cos(wave_number * radius) / radius)
        imag_part = np.where(inside, 0.0, near_scale * np.sin(wave_number * radius) / radius)
        blocks.append(np.concatenate([real_part, imag_part], axis=0))
    return np.stack(blocks).astype(np.float32)


def pair_tables():
    slab_of, pos_of, valid, flips = [], [], [], []
    for base in range(8):
        bx, by, bz = base // 4, base // 2 % 2, base % 2
        for target in range(CY * CZ):
            ty, tz = target // CZ, target % CZ
            for side in range(2):
                shift_x = 0 if bx == 0 else (1 if side == 0 else -1)
                slab_of.append(1 + shift_x)
                pos_of.append((ty ^ by) * CZ + (tz ^ bz))
                valid.append(1.0 if (bx == 1 or side == 0) else 0.0)
                flips.append((shift_x < 0, by == 1 and ty == 1, bz == 1 and tz == 1))
    return (np.array(slab_of), np.array(pos_of), np.array(valid, np.float32), np.array(flips))


def flip_matrices():
    index = np.arange(V)
    coords = [index // (BSIDE * BSIDE), index // BSIDE % BSIDE, index % BSIDE]
    matrices = []
    for dimension in range(3):
        moved = list(coords)
        moved[dimension] = BSIDE - 1 - coords[dimension]
        source = moved[0] * BSIDE * BSIDE + moved[1] * BSIDE + moved[2]
        matrices.append((source[None, :] == index[:, None]).astype(np.float32))
    return matrices


def masked_flips(rows, masks, precision):
    for matrix, mask in zip(flip_matrices(), masks):
        flipped = jnp.dot(
            rows, jnp.asarray(matrix, rows.dtype), precision=precision,
            preferred_element_type=jnp.float32,
        ).astype(rows.dtype)
        rows = jnp.where(mask[:, None], flipped, rows)
    return rows


def near_field(sources, box_pos):
    exc_dev = sources.shape[1]
    box_dev = sources.shape[2]
    slots = CY * CZ
    extended = padded(sources, (("box", 2),), box_dev)
    zeros_pos = jnp.zeros((box_dev,), jnp.int32)
    padded_pos = jnp.concatenate([zeros_pos, box_pos, zeros_pos])
    local_pos = lax.dynamic_slice_in_dim(padded_pos, lax.axis_index("box") * box_dev, 3 * box_dev)
    slab_of, pos_of, valid, flips = pair_tables()
    column_slab = np.arange(3 * box_dev) // box_dev
    selector = (
        (slab_of[:, None] == column_slab[None, :])
        & (pos_of[:, None] == local_pos[None, :])
    ).astype(jnp.float32) * valid[:, None]
    selector = selector.reshape(8, 1, slots, 2, 1, 1, 1, 3 * box_dev)
    part_eye = np.eye(2, dtype=np.float32).reshape(1, 2, 1, 1, 1, 2, 1, 1)
    exc_eye = np.eye(exc_dev, dtype=np.float32).reshape(1, 1, 1, 1, exc_dev, 1, exc_dev, 1)
    gather = (selector * part_eye * exc_eye).reshape(-1, 2 * exc_dev * 3 * box_dev)
    pieces = jnp.dot(
        gather.astype(jnp.bfloat16), extended.reshape(-1, V), preferred_element_type=jnp.float32
    ).astype(jnp.bfloat16)
    row_flips = np.broadcast_to(
        flips.reshape(8, 1, slots, 2, 1, 3), (8, 2, slots, 2, exc_dev, 3)
    ).reshape(-1, 3)
    masks = [row_flips[:, d] for d in range(3)]
    pieces = masked_flips(pieces, masks, None)
    blocks = jnp.asarray(green_constants(), jnp.bfloat16)
    product = lax.dot_general(
        pieces.reshape(8, -1, V), blocks, (((2,), (2,)), ((0,), (0,))),
        preferred_element_type=jnp.float32,
    )
    product = product.reshape(8, 2, -1, 2, V)
    result = jnp.stack(
        [
            product[:, 0, :, 0] - product[:, 1, :, 1],
            product[:, 0, :, 1] + product[:, 1, :, 0],
        ],
        axis=1,
    ).reshape(-1, V)
    result = masked_flips(result, masks, lax.Precision.HIGHEST)
    own_pos = local_pos[box_dev : 2 * box_dev]
    choose = (own_pos[:, None] == jnp.arange(slots, dtype=jnp.int32)[None, :]).astype(jnp.float32)
    choose = choose.reshape(1, 1, box_dev, 1, 1, slots, 1, 1)
    part_eye = np.eye(2, dtype=np.float32).reshape(2, 1, 1, 1, 2, 1, 1, 1)
    exc_eye = np.eye(exc_dev, dtype=np.float32).reshape(1, exc_dev, 1, 1, 1, 1, 1, exc_dev)
    ones = np.ones((1, 1, 1, 8, 1, 1, 2, 1), np.float32)
    summing = (choose * part_eye * exc_eye * ones).reshape(2 * exc_dev * box_dev, -1)
    placed = jnp.dot(summing, result, precision=lax.Precision.HIGHEST)
    return placed.reshape(2, exc_dev, box_dev, V)


def encode(sources, enc_table):
    real_prod = jnp.einsum(
        "kv,xebv->kxeb", enc_table[0], sources, preferred_element_type=jnp.float32
    )
    imag_prod = jnp.einsum(
        "kv,xebv->kxeb", enc_table[1], sources, preferred_element_type=jnp.float32
    )
    return jnp.stack(
        [real_prod[:, 0] - imag_prod[:, 1], imag_prod[:, 0] + real_prod[:, 1]], axis=1
    ).astype(jnp.bfloat16)


def translate(encoded, translators):
    real_prod = jnp.einsum(
        "kts,kxes->kxet", translators[:, 0], encoded, preferred_element_type=jnp.float32
    )
    imag_prod = jnp.einsum(
        "kts,kxes->kxet", translators[:, 1], encoded, preferred_element_type=jnp.float32
    )
    return jnp.stack(
        [real_prod[:, 0] - imag_prod[:, 1], imag_prod[:, 0] + real_prod[:, 1]], axis=1
    ).astype(jnp.bfloat16)


def decode(returned, dec_table):
    real_prod = jnp.einsum(
        "vk,kxeb->xebv", dec_table[0], returned, preferred_element_type=jnp.float32
    )
    imag_prod = jnp.einsum(
        "vk,kxeb->xebv", dec_table[1], returned, preferred_element_type=jnp.float32
    )
    return jnp.stack([real_prod[0] - imag_prod[1], imag_prod[0] + real_prod[1]])


def shards(incident, contrast, box_pos, directions, enc_table, dec_table):
    contrast_real = contrast.astype(jnp.float32) * chi_step
    translators = build_translators(directions, box_pos)
    fields = incident
    outputs = []
    for term_index in range(2):
        sources = (contrast_real[None, None] * fields.astype(jnp.float32)).astype(jnp.bfloat16)
        near_part = near_field(sources, box_pos)
        encoded = encode(sources, enc_table)
        returned = lax.all_to_all(
            translate(
                lax.all_to_all(encoded, "box", split_axis=0, concat_axis=3, tiled=True), translators
            ),
            "box",
            split_axis=3,
            concat_axis=0,
            tiled=True,
        )
        fields = (near_part + decode(returned, dec_table)).astype(jnp.bfloat16)
        outputs.append(fields)
    first_sq = jnp.sum(jnp.square(outputs[0].astype(jnp.float32)), axis=(0, 1, 3))
    second_sq = jnp.sum(jnp.square(outputs[1].astype(jnp.float32)), axis=(0, 1, 3))
    first_sum, second_sum = lax.psum((first_sq, second_sq), "exc")
    entry_count = 2 * outputs[0].shape[1] * lax.axis_size("exc") * outputs[0].shape[3]
    series_ratio = jnp.sqrt(second_sum / entry_count / (first_sum / entry_count + epsilon))
    return (outputs[0], outputs[1], series_ratio)


def solution(mesh):
    placed = (P(None, "exc", "box", None), P("box", None), P(), P(None, "box"), P(), P())
    return jax.shard_map(
        shards,
        mesh=mesh,
        in_specs=placed,
        out_specs=(P(None, "exc", "box", None), P(None, "exc", "box", None), P("box")),
        check_vma=False,
    )
```

profile of v0, /device:TPU:1, one launch (start us, length us, event | category | flops | bytes accessed | tf_op | source)
XLA Modules:
  0.0 214.1 jit_solution(10312666330083657233)
XLA Ops:
  3.4 5.4 %collective-permute-start = (bf16[2,2,4,512]{3,2,1,0:T(4,128)(2,1)S(1)}, bf16[2,2,4,512]{3,2,1,0:T(4,128)(2,1)S(1)}, u32[]{:S(2)}, u32[]{:S(2)}) collective-permute-start(bf16[2,2,4,512]{3,2,1,0:T(4,128)(2,1)S(1)} %multiply_convert_fusion.3), channel_id=1, source_target_pairs={{0,4},{4,8},{8,12},{12,16},{16,20},{20,24},{24,28},{28,32},{32,36}... | collective-permute-start | bytes 49160 | tf_op jit(solution)/shard_map/ppermute | solution.py:26
  12.6 22.5 %all-to-all-start = ((bf16[512,2,2,4]{3,2,1,0:T(2,128)(2,1)}), bf16[512,2,2,4]{3,2,1,0:T(2,128)(2,1)}, u32[]{:S(2)}, u32[]{:S(2)}) async-start(bf16[512,2,2,4]{3,2,1,0:T(2,128)(2,1)} %copy.104), calls=%async_computation | async-start | bytes 1048576 | tf_op jit(solution)/shard_map/all_to_all | solution.py:250
  41.6 5.4 %fusion.33 = (f32[512,512]{1,0:T(8,128)S(1)}, f32[512,512]{1,0:T(8,128)S(1)}, f32[512,512]{1,0:T(8,128)S(1)}, f32[512,512]{1,0:T(8,128)S(1)}, f32[512,512]{1,0:T...) fusion(f32[512]{0:T(512)S(1)} %get-tuple-element.47, ...), kind=kLoop, calls=%fused_computation.83 | loop fusion | flops 10747904 | bytes 14686208 | tf_op jit(solution)/shard_map/vmap()/neg | solution.py:54
  47.0 5.2 %multiply_convert_fusion.1 = (bf16[1,4,512,512]{3,2,1,0:T(8,128)(2,1)S(1)}, bf16[1,4,512,512]{3,2,1,0:T(8,128)(2,1)S(1)}) fusion(f32[512,512]{1,0:T(8,128)S(1)} %get-tuple-element.38, f32[512,512]{1,0:T(8,128)S(1)} %get-tuple-element.39, f32[512,512]{1,0:T(8,128)S(1)} %get-tuple-element.37, f32[512,512]{1,0:T(8,128)S(1)} %get-tuple-element.32, ...), kind=kLoop, calls=%fused_computation.4 | loop fusion | flops 36700160 | bytes 18874416 | tf_op jit(solution)/shard_map/convert.6
  52.3 2.3 %maximum_bitcast_fusion = bf16[4,2,512,512]{3,2,0,1:T(8,128)(2,1)} fusion(bf16[1,4,512,512]{3,2,1,0:T(8,128)(2,1)S(1)} %get-tuple-element.6, bf16[1,4,512,512]{3,2,1,0:T(8,128)(2,1)S(1)} %get-tuple-element.5), kind=kLoop, calls=%fused_computation.2 | loop fusion | flops 2097152 | bytes 8388608 | tf_op jit(solution)/shard_map/vmap()/transpose | solution.py:96
  56.1 5.9 %fusion.67 = f32[8,32,1024]{2,1,0:T(8,128)S(1)} fusion(bf16[8,32,512]{2,1,0:T(8,128)(2,1)S(1)} %bitcast.178, bf16[8,1024,512]{2,1,0:T(8,128)(2,1)} %constant.138.clone), kind=kOutput, calls=%fused_computation.166 | convolution fusion | flops 268435456 | bytes 9699328 | tf_op jit(solution)/shard_map/dot_general | solution.py:181
  62.0 1.9 reshape.1232
  63.9 2.7 %fusion.66 = (f32[8,1,16,1,512]{4,3,2,1,0:T(1,128)S(1)}, f32[8,1,16,1,512]{4,3,2,1,0:T(1,128)S(1)}, f32[8,1,16,1,512]{4,3,2,1,0:T(1,128)S(1)}, f32[8,1,16,1,512]{4,3,2,1,0:T(1,128)S(1)}) fusion(f32[8,2,16,2,512]{4,3,2,1,0:T(2,128)} %reshape.1232), kind=kLoop, calls=%fused_computation.165 | loop fusion | bytes 2097152 | tf_op jit(solution)/shard_map/slice | solution.py:188
  67.9 1.9 convolution_select_fusion.4
  71.8 2.3 %fusion.4 = f32[4,2,2,512]{3,2,1,0:T(2,128)S(1)} fusion(bf16[4,2,2,512]{3,2,1,0:T(2,128)(2,1)S(1)} %all_to_all.55, bf16[4,2,512,512]{3,2,0,1:T(8,128)(2,1)} %maximum_bitcast_fusion), kind=kOutput, calls=%fused_computation.14 | convolution fusion | flops 8388608 | bytes 2146304 | tf_op jit(solution)/shard_map/kts,kxes->kxet/dot_general | solution.py:221
  74.1 2.3 %fusion.2 = f32[4,2,2,512]{3,2,1,0:T(2,128)S(1)} fusion(bf16[4,2,2,512]{3,2,1,0:T(2,128)(2,1)S(1)} %all_to_all.55, bf16[4,2,512,512]{3,2,0,1:T(8,128)(2,1)} %maximum_bitcast_fusion), kind=kOutput, calls=%fused_computation.12 | convolution fusion | flops 8388608 | bytes 2146304 | tf_op jit(solution)/shard_map/kts,kxes->kxet/dot_general | solution.py:218
  77.6 14.3 %all-to-all-start.1 = ((bf16[4,2,2,512]{0,2,1,3:T(2,128)(2,1)}), bf16[4,2,2,512]{0,2,1,3:T(2,128)(2,1)}, u32[]{:S(2)}, u32[]{:S(2)}) async-start(bf16[4,2,2,512]{0,2,1,3:T(2,128)(2,1)} %copy.107), calls=%async_computation.1 | async-start | bytes 1048576 | tf_op jit(solution)/shard_map/all_to_all | solution.py:248
  92.0 3.1 %fusion.5 = f32[256,512,1,1]{1,0,3,2:T(8,128)} fusion(f32[256,512]{1,0:T(8,128)} %convolution_select_fusion.4, f32[512,512]{1,0:T(8,128)S(1)} %copy-done, pred[256]{0:T(512)(128)(4,1)S(1)} %copy-done.6), kind=kOutput, calls=%fused_computation.22 | convolution fusion | flops 805437440 | bytes 2097408 | tf_op jit(solution)/shard_map/dot_general | solution.py:146
  95.0 13.9 %all-to-all-done.1 = bf16[4,2,2,512]{0,2,1,3:T(2,128)(2,1)} async-done(((bf16[4,2,2,512]{0,2,1,3:T(2,128)(2,1)}), bf16[4,2,2,512]{0,2,1,3:T(2,128)(2,1)}, u32[]{:S(2)}, u32[]{:S(2)}) %all-to-all-start.1) | async-done | bytes 16416 | tf_op jit(solution)/shard_map/all_to_all | solution.py:248
  108.9 2.0 copy.169
  110.9 1.8 all_to_all.59
  113.5 2.7 %fusion.47 = (f32[4]{0:T(128)S(1)}, bf16[2,2,4,512]{3,2,1,0:T(4,128)(2,1)S(1)}, bf16[2,2,4,512]{3,2,1,0:T(4,128)(2,1)}) fusion(f32[4,512]{1,0:T(4,128)S(1)} %convert_multiply_fusion.2, f32[1,2,4,512]{3,2,1,0:T(4,128)S(1)} %get-tuple-element.22, f32[1,2,4,512]{3,2,1,0:T(4,128)S(1)} %get-tuple-element.21, f32[2,2,4,256]{2,3,1,0:T(8,128)S(1)} %bitcast.169, ...), kind=kOutput, calls=%fused_computation.107 | convolution fusion | flops 25231356 | bytes 614416 | tf_op jit(solution)/shard_map/dot_general | solution.py:201
  120.1 4.0 %collective-permute-start.2 = (bf16[2,2,4,512]{3,2,1,0:T(4,128)(2,1)S(1)}, bf16[2,2,4,512]{3,2,1,0:T(4,128)(2,1)S(1)}, u32[]{:S(2)}, u32[]{:S(2)}) collective-permute-start(bf16[2,2,4,512]{3,2,1,0:T(4,128)(2,1)S(1)} %get-tuple-element.28), channel_id=1, source_target_pairs={{0,4},{4,8},{8,12},{12,16},{16,20},{20,24},{24,28},{28,32},{32,36}... | collective-permute-start | bytes 49160 | tf_op jit(solution)/shard_map/ppermute | solution.py:26
  125.3 12.9 %all-to-all-start.2 = ((bf16[512,2,2,4]{3,2,1,0:T(2,128)(2,1)}), bf16[512,2,2,4]{3,2,1,0:T(2,128)(2,1)}, u32[]{:S(2)}, u32[]{:S(2)}) async-start(bf16[512,2,2,4]{3,2,1,0:T(2,128)(2,1)} %copy.115), calls=%async_computation.2 | async-start | bytes 1048576 | tf_op jit(solution)/shard_map/all_to_all | solution.py:250
  138.5 1.3 fusion.9
  139.8 1.3 fusion.8
  141.2 1.3 fusion.7
  142.5 6.9 %fusion.68 = f32[8,32,1024]{2,1,0:T(8,128)} fusion(bf16[8,32,512]{2,1,0:T(8,128)(2,1)S(1)} %bitcast.177, bf16[8,1024,512]{2,1,0:T(8,128)(2,1)} %constant.138.clone), kind=kOutput, calls=%fused_computation.167 | convolution fusion | flops 268435456 | bytes 9699328 | tf_op jit(solution)/shard_map/dot_general | solution.py:181
  149.5 3.1 %reshape.1236 = f32[8,2,16,2,512]{4,3,2,1,0:T(2,128)} reshape(f32[8,32,1024]{2,1,0:T(8,128)} %fusion.68) | data formatting | bytes 2097152 | tf_op jit(solution)/shard_map/reshape | solution.py:185
  152.6 2.8 %fusion.65 = (f32[8,1,16,1,512]{4,3,2,1,0:T(1,128)S(1)}, f32[8,1,16,1,512]{4,3,2,1,0:T(1,128)S(1)}, f32[8,1,16,1,512]{4,3,2,1,0:T(1,128)S(1)}, f32[8,1,16,1,512]{4,3,2,1,0:T(1,128)S(1)}) fusion(f32[8,2,16,2,512]{4,3,2,1,0:T(2,128)} %reshape.1236), kind=kLoop, calls=%fused_computation.164 | loop fusion | bytes 2097152 | tf_op jit(solution)/shard_map/slice | solution.py:188
  159.6 2.3 %fusion.3 = f32[4,2,2,512]{3,2,1,0:T(2,128)S(1)} fusion(bf16[4,2,2,512]{3,2,1,0:T(2,128)(2,1)S(1)} %all_to_all.63, bf16[4,2,512,512]{3,2,0,1:T(8,128)(2,1)} %maximum_bitcast_fusion), kind=kOutput, calls=%fused_computation.13 | convolution fusion | flops 8388608 | bytes 2146304 | tf_op jit(solution)/shard_map/kts,kxes->kxet/dot_general | solution.py:221
  161.9 2.3 %fusion.1 = f32[4,2,2,512]{3,2,1,0:T(2,128)S(1)} fusion(bf16[4,2,2,512]{3,2,1,0:T(2,128)(2,1)S(1)} %all_to_all.63, bf16[4,2,512,512]{3,2,0,1:T(8,128)(2,1)} %maximum_bitcast_fusion), kind=kOutput, calls=%fused_computation.11 | convolution fusion | flops 8388608 | bytes 2146304 | tf_op jit(solution)/shard_map/kts,kxes->kxet/dot_general | solution.py:218
  165.5 14.3 %all-to-all-start.3 = ((bf16[4,2,2,512]{0,2,1,3:T(2,128)(2,1)}), bf16[4,2,2,512]{0,2,1,3:T(2,128)(2,1)}, u32[]{:S(2)}, u32[]{:S(2)}) async-start(bf16[4,2,2,512]{0,2,1,3:T(2,128)(2,1)} %copy.118), calls=%async_computation.3 | async-start | bytes 1048576 | tf_op jit(solution)/shard_map/all_to_all | solution.py:248
  179.8 1.9 fusion.6
  181.7 14.9 %all-to-all-done.3 = bf16[4,2,2,512]{0,2,1,3:T(2,128)(2,1)} async-done(((bf16[4,2,2,512]{0,2,1,3:T(2,128)(2,1)}), bf16[4,2,2,512]{0,2,1,3:T(2,128)(2,1)}, u32[]{:S(2)}, u32[]{:S(2)}) %all-to-all-start.3) | async-done | bytes 16416 | tf_op jit(solution)/shard_map/all_to_all | solution.py:248
  199.1 2.7 %multiply_reduce_fusion = (f32[4]{0:T(128)S(1)}, bf16[2,2,4,512]{3,2,1,0:T(4,128)(2,1)}) fusion(f32[1,2,4,512]{3,2,1,0:T(4,128)S(1)} %get-tuple-element.16, f32[1,2,4,512]{3,2,1,0:T(4,128)S(1)} %get-tuple-element.15, f32[2,2,4,256]{2,3,1,0:T(8,128)S(1)} %bitcast.170, f32[256,512,1,1]{1,0,3,2:T(8,128)} %fusion.6), kind=kOutput, calls=%fused_computation.108 | convolution fusion | flops 25214972 | bytes 589840 | tf_op jit(solution)/shard_map/dot_general | solution.py:201
  201.8 11.7 %all-reduce = (f32[4]{0:T(128)S(1)}, f32[4]{0:T(128)S(1)}) all-reduce(f32[4]{0:T(128)S(1)} %get-tuple-element.27, f32[4]{0:T(128)S(1)} %get-tuple-element.49), channel_id=1, replica_groups=mesh['box'=128,'exc'=4] {'exc'}, use_global_device_ids=true, to_apply=%region_3.4 | all-reduce | flops 8 | bytes 64 | tf_op jit(solution)/shard_map/psum | solution.py:261
  (94 shorter events, 33.3 us)
Async XLA Ops:
  2.1 52.8 %collective-permute-start.1 = (bf16[2,2,4,512]{3,2,1,0:T(4,128)(2,1)S(1)}, bf16[2,2,4,512]{3,2,1,0:T(4,128)(2,1)S(1)}, u32[]{:S(2)}, u32[]{:S(2)}) collective-permute-start(bf16[2,2,4,512]{3,2,1,0:T(4,128)(2,1)S(1)} %multiply_convert_fusion.3), channel_id=1, source_target_pairs={{4,0},{8,4},{12,8},{16,12},{20,16},{24,20},{28,24},{32,28},{36,32}... | collective-permute-start | bytes 49160 | tf_op jit(solution)/shard_map/ppermute | solution.py:29
  3.4 51.5 %collective-permute-start = (bf16[2,2,4,512]{3,2,1,0:T(4,128)(2,1)S(1)}, bf16[2,2,4,512]{3,2,1,0:T(4,128)(2,1)S(1)}, u32[]{:S(2)}, u32[]{:S(2)}) collective-permute-start(bf16[2,2,4,512]{3,2,1,0:T(4,128)(2,1)S(1)} %multiply_convert_fusion.3), channel_id=1, source_target_pairs={{0,4},{4,8},{8,12},{12,16},{16,20},{20,24},{24,28},{28,32},{32,36}... | collective-permute-start | bytes 49160 | tf_op jit(solution)/shard_map/ppermute | solution.py:26
  12.6 57.1 %all-to-all-start = ((bf16[512,2,2,4]{3,2,1,0:T(2,128)(2,1)}), bf16[512,2,2,4]{3,2,1,0:T(2,128)(2,1)}, u32[]{:S(2)}, u32[]{:S(2)}) async-start(bf16[512,2,2,4]{3,2,1,0:T(2,128)(2,1)} %copy.104), calls=%async_computation | async-start | bytes 1048576 | tf_op jit(solution)/shard_map/all_to_all | solution.py:250
  52.2 2.9 %copy-start.8 = (pred[256]{0:T(512)(128)(4,1)S(1)}, pred[256]{0:T(512)(128)(4,1)}, u32[]{:S(2)}) copy-start(pred[256]{0:T(512)(128)(4,1)} %constant.152) | copy-start | bytes 772
  52.3 2.9 %copy-start.11 = (bf16[512,512]{1,0:T(8,128)(2,1)S(1)}, bf16[512,512]{1,0:T(8,128)(2,1)}, u32[]{:S(2)}) copy-start(bf16[512,512]{1,0:T(8,128)(2,1)} %constant.132.clone) | copy-start | bytes 1572868
  52.3 3.2 %copy-start.7 = (pred[256]{0:T(512)(128)(4,1)S(1)}, pred[256]{0:T(512)(128)(4,1)}, u32[]{:S(2)}) copy-start(pred[256]{0:T(512)(128)(4,1)} %constant.151) | copy-start | bytes 772
  52.3 3.2 %copy-start.10 = (bf16[512,512]{1,0:T(8,128)(2,1)S(1)}, bf16[512,512]{1,0:T(8,128)(2,1)}, u32[]{:S(2)}) copy-start(bf16[512,512]{1,0:T(8,128)(2,1)} %constant.134.clone) | copy-start | bytes 1572868
  52.3 3.5 %copy-start.6 = (pred[256]{0:T(512)(128)(4,1)S(1)}, pred[256]{0:T(512)(128)(4,1)}, u32[]{:S(2)}) copy-start(pred[256]{0:T(512)(128)(4,1)} %constant.150) | copy-start | bytes 772
  52.3 3.5 %copy-start.9 = (bf16[512,512]{1,0:T(8,128)(2,1)S(1)}, bf16[512,512]{1,0:T(8,128)(2,1)}, u32[]{:S(2)}) copy-start(bf16[512,512]{1,0:T(8,128)(2,1)} %constant.136.clone) | copy-start | bytes 1572868
  62.0 4.8 %copy-start.2 = (f32[512,512]{1,0:T(8,128)S(1)}, f32[512,512]{1,0:T(8,128)}, u32[]{:S(2)}) copy-start(f32[512,512]{1,0:T(8,128)} %constant.139.clone) | copy-start | bytes 3145732
  62.0 5.9 %copy-start.1 = (f32[512,512]{1,0:T(8,128)S(1)}, f32[512,512]{1,0:T(8,128)}, u32[]{:S(2)}) copy-start(f32[512,512]{1,0:T(8,128)} %constant.140.clone) | copy-start | bytes 3145732
  69.7 22.2 %copy-start = (f32[512,512]{1,0:T(8,128)S(1)}, f32[512,512]{1,0:T(8,128)}, u32[]{:S(2)}) copy-start(f32[512,512]{1,0:T(8,128)} %constant.141.clone) | copy-start | bytes 3145732
  74.1 38.7 %copy-start.4 = (bf16[2,512,512]{2,1,0:T(8,128)(2,1)S(1)}, bf16[2,512,512]{2,1,0:T(8,128)(2,1)}, u32[]{:S(2)}) copy-start(bf16[2,512,512]{2,1,0:T(8,128)(2,1)} %param.53) | copy-start | bytes 3145732
  77.6 31.2 %all-to-all-start.1 = ((bf16[4,2,2,512]{0,2,1,3:T(2,128)(2,1)}), bf16[4,2,2,512]{0,2,1,3:T(2,128)(2,1)}, u32[]{:S(2)}, u32[]{:S(2)}) async-start(bf16[4,2,2,512]{0,2,1,3:T(2,128)(2,1)} %copy.107), calls=%async_computation.1 | async-start | bytes 1048576 | tf_op jit(solution)/shard_map/all_to_all | solution.py:248
  118.8 19.4 %collective-permute-start.3 = (bf16[2,2,4,512]{3,2,1,0:T(4,128)(2,1)S(1)}, bf16[2,2,4,512]{3,2,1,0:T(4,128)(2,1)S(1)}, u32[]{:S(2)}, u32[]{:S(2)}) collective-permute-start(bf16[2,2,4,512]{3,2,1,0:T(4,128)(2,1)S(1)} %get-tuple-element.28), channel_id=1, source_target_pairs={{4,0},{8,4},{12,8},{16,12},{20,16},{24,20},{28,24},{32,28},{36,32}... | collective-permute-start | bytes 49160 | tf_op jit(solution)/shard_map/ppermute | solution.py:29
  120.1 18.1 %collective-permute-start.2 = (bf16[2,2,4,512]{3,2,1,0:T(4,128)(2,1)S(1)}, bf16[2,2,4,512]{3,2,1,0:T(4,128)(2,1)S(1)}, u32[]{:S(2)}, u32[]{:S(2)}) collective-permute-start(bf16[2,2,4,512]{3,2,1,0:T(4,128)(2,1)S(1)} %get-tuple-element.28), channel_id=1, source_target_pairs={{0,4},{4,8},{8,12},{12,16},{16,20},{20,24},{24,28},{28,32},{32,36}... | collective-permute-start | bytes 49160 | tf_op jit(solution)/shard_map/ppermute | solution.py:26
  125.3 32.3 %all-to-all-start.2 = ((bf16[512,2,2,4]{3,2,1,0:T(2,128)(2,1)}), bf16[512,2,2,4]{3,2,1,0:T(2,128)(2,1)}, u32[]{:S(2)}, u32[]{:S(2)}) async-start(bf16[512,2,2,4]{3,2,1,0:T(2,128)(2,1)} %copy.115), calls=%async_computation.2 | async-start | bytes 1048576 | tf_op jit(solution)/shard_map/all_to_all | solution.py:250
  152.6 2.9 %copy-start.3 = (f32[512,512]{1,0:T(8,128)S(1)}, f32[512,512]{1,0:T(8,128)}, u32[]{:S(2)}) copy-start(f32[512,512]{1,0:T(8,128)} %constant.139.clone) | copy-start | bytes 3145732
  161.9 36.7 %copy-start.5 = (bf16[2,512,512]{2,1,0:T(8,128)(2,1)S(1)}, bf16[2,512,512]{2,1,0:T(8,128)(2,1)}, u32[]{:S(2)}) copy-start(bf16[2,512,512]{2,1,0:T(8,128)(2,1)} %param.53) | copy-start | bytes 3145732
  165.5 31.1 %all-to-all-start.3 = ((bf16[4,2,2,512]{0,2,1,3:T(2,128)(2,1)}), bf16[4,2,2,512]{0,2,1,3:T(2,128)(2,1)}, u32[]{:S(2)}, u32[]{:S(2)}) async-start(bf16[4,2,2,512]{0,2,1,3:T(2,128)(2,1)} %copy.118), calls=%async_computation.3 | async-start | bytes 1048576 | tf_op jit(solution)/shard_map/all_to_all | solution.py:248
where the time goes:
time: 216 us; the launch traced here: 214 us
  starting transfers between devices  76 us (35%)
  matrix products  49 us (23%)
  waiting for transfers between devices  28.8 us (13%)
  local copies, waits for them, and re-layouts  26.4 us (12%)
  other arithmetic  20.9 us (10%)
  blocking collectives  11.7 us (5%)
    all_to_all x2, starting transfers between devices, shards(): lax.all_to_all(encoded, 'box', split_axis=0, concat_axis=3, tiled=True)  35.4 us
    all_to_all x2, waiting for transfers between devices, shards(): lax.all_to_all(translate(lax.all_to_all(encoded, 'box', split_axis=0, con...  28.8 us
    all_to_all x2, starting transfers between devices, shards(): lax.all_to_all(translate(lax.all_to_all(encoded, 'box', split_axis=0, con...  28.6 us
    dot_general x12, matrix products, masked_flips(): jnp.dot(rows, jnp.asarray(matrix, rows.dtype), precision=precision, prefe...  14.9 us
    dot_general x2, matrix products, near_field(): lax.dot_general(pieces.reshape(8, -1, V), blocks, (((2,), (2,)), ((0,), (...  12.8 us
    psum x1, blocking collectives, shards(): first_sum, second_sum = lax.psum((first_sq, second_sq), 'exc')  11.7 us
    ppermute x2, starting transfers between devices, padded(): lax.ppermute(lax.slice_in_dim(block, block.shape[dim] - width, None, axis...  9.43 us
    all_to_all x4, local copies, waits for them, and re-layouts, shards(): lax.all_to_all(translate(lax.all_to_all(encoded, 'box', split_axis=0, con...  5.8 us
  transfers between devices with their start and end apart: 8, of which 2 were waited for; matrix products, arithmetic and copies ran while one was open for 30% of the time, Pallas kernels for 0%

commit v1 on v0

--- a/solution.py
+++ b/solution.py
@@ -39,10 +39,10 @@
     return (slab_coord, row_coord, col_coord)
 
 
-def translator(column, coords):
-    slab_gap = coords[0][:, None] - coords[0][None, :]
-    row_gap = coords[1][:, None] - coords[1][None, :]
-    col_gap = coords[2][:, None] - coords[2][None, :]
+def translator(column, targets, coords):
+    slab_gap = targets[0][:, None] - coords[0][None, :]
+    row_gap = targets[1][:, None] - coords[1][None, :]
+    col_gap = targets[2][:, None] - coords[2][None, :]
     square = slab_gap * slab_gap + row_gap * row_gap + col_gap * col_gap
     nearby = jnp.maximum(jnp.maximum(jnp.abs(slab_gap), jnp.abs(row_gap)), jnp.abs(col_gap)) < 1.5
     radius = jnp.sqrt(jnp.maximum(square, 1.0))
@@ -87,13 +87,15 @@
     return jnp.stack([real_part, imag_part]).astype(jnp.bfloat16)
 
 
-def build_translators(dir_block, box_pos):
+def build_translators(columns, box_pos, box_dev):
     coords = box_coords(box_pos)
+    first = lax.axis_index("box") * box_dev
+    targets = tuple(lax.dynamic_slice_in_dim(part, first, box_dev) for part in coords)
 
     def one_direction(column):
-        return translator(column, coords)
-
-    return jax.vmap(one_direction)(jnp.transpose(dir_block))
+        return translator(column, targets, coords)
+
+    return jax.vmap(one_direction)(columns)
 
 
 def green_constants():
@@ -216,10 +218,10 @@
 
 def translate(encoded, translators):
     real_prod = jnp.einsum(
-        "kts,kxes->kxet", translators[:, 0], encoded, preferred_element_type=jnp.float32
+        "kts,skxe->kxet", translators[:, 0], encoded, preferred_element_type=jnp.float32
     )
     imag_prod = jnp.einsum(
-        "kts,kxes->kxet", translators[:, 1], encoded, preferred_element_type=jnp.float32
+        "kts,skxe->kxet", translators[:, 1], encoded, preferred_element_type=jnp.float32
     )
     return jnp.stack(
         [real_prod[:, 0] - imag_prod[:, 1], imag_prod[:, 0] + real_prod[:, 1]], axis=1
@@ -238,22 +240,17 @@
 
 def shards(incident, contrast, box_pos, directions, enc_table, dec_table):
     contrast_real = contrast.astype(jnp.float32) * chi_step
-    translators = build_translators(directions, box_pos)
+    columns = lax.all_gather(jnp.transpose(directions), "box", axis=0, tiled=True)
+    translators = build_translators(columns, box_pos, contrast.shape[0])
     fields = incident
     outputs = []
     for term_index in range(2):
         sources = (contrast_real[None, None] * fields.astype(jnp.float32)).astype(jnp.bfloat16)
         near_part = near_field(sources, box_pos)
         encoded = encode(sources, enc_table)
-        returned = lax.all_to_all(
-            translate(
-                lax.all_to_all(encoded, "box", split_axis=0, concat_axis=3, tiled=True), translators
-            ),
-            "box",
-            split_axis=3,
-            concat_axis=0,
-            tiled=True,
-        )
+        by_box = jnp.transpose(encoded, (3, 0, 1, 2))
+        gathered = lax.all_gather(by_box, "box", axis=0, tiled=True)
+        returned = translate(gathered, translators)
         fields = (near_part + decode(returned, dec_table)).astype(jnp.bfloat16)
         outputs.append(fields)
     first_sq = jnp.sum(jnp.square(outputs[0].astype(jnp.float32)), axis=(0, 1, 3))

time: 216 us -> 1480 us (6.85)
  waiting for transfers between devices: 28.8 us -> 914 us
  blocking collectives: 11.7 us -> 422 us
  starting transfers between devices: 76 us -> 8.99 us
  local copies, waits for them, and re-layouts: 26.4 us -> 42.2 us
    all_gather x0 -> x2, waiting for transfers between devices: none -> 911 us  [shards(): gathered = lax.all_gather(by_box, 'box', axis=0, tiled=True)]
    all_gather x0 -> x1, blocking collectives: none -> 319 us  [shards(): lax.all_gather(jnp.transpose(directions), 'box', axis=0, tiled=True)]
    psum x1, blocking collectives: 11.7 us -> 102 us  [shards(): first_sum, second_sum = lax.psum((first_sq, second_sq), 'exc')]
    all_to_all x4 -> x0, starting transfers between devices: 64 us -> none  [the longest x2 35.4 us: shards(): lax.all_to_all(encoded, 'box', split_axis=0, concat_axis=3, tiled=True)]
    all_to_all x4 -> x0, waiting for transfers between devices: 28.8 us -> none  [the longest x2 28.8 us: shards(): lax.all_to_all(translate(lax.all_to_all(encoded, 'box', split_axis=0, con...]
    all_gather x0 -> x2, local copies, waits for them, and re-layouts: none -> 21 us  [shards(): gathered = lax.all_gather(by_box, 'box', axis=0, tiled=True)]
  transfers between devices with their start and end apart: 8 -> 6, of which waited for: 2 -> 3; matrix products, arithmetic and copies ran while one was open for 30% -> 4% of each run, Pallas kernels for 0% -> 0%
where the time goes in v1:
time: 1480 us
  waiting for transfers between devices  914 us (62%)
  blocking collectives  422 us (29%)
  matrix products  56.9 us (4%)
  local copies, waits for them, and re-layouts  42.2 us (3%)
  other arithmetic  21.1 us (1%)
    all_gather x2, waiting for transfers between devices, shards(): gathered = lax.all_gather(by_box, 'box', axis=0, tiled=True)  911 us
    all_gather x1, blocking collectives, shards(): lax.all_gather(jnp.transpose(directions), 'box', axis=0, tiled=True)  319 us
    psum x1, blocking collectives, shards(): first_sum, second_sum = lax.psum((first_sq, second_sq), 'exc')  102 us
  transfers between devices with their start and end apart: 6, of which 3 were waited for; matrix products, arithmetic and copies ran while one was open for 4% of the time, Pallas kernels for 0%

profile of v1, /device:TPU:1, one launch (start us, length us, event | category | flops | bytes accessed | tf_op | source)
XLA Modules:
  0.0 1480.0 jit_solution(3429541282478494032)
XLA Ops:
  8.7 4.8 collective-permute-start
  14.8 1.3 convolution_bitcast_fusion.2
  16.1 1.3 convolution_bitcast_fusion.3
  20.6 319.5 %all-gather = f32[128,4,3]{2,1,0:T(4,128)S(1)} all-gather(f32[1,4,3]{2,1,0:T(4,128)S(1)} %bitcast.147), channel_id=1, replica_groups=mesh['box'=128,'exc'=4] {'box'}, dimensions={0}, use_global_device_ids=true | all-gather | bytes 6192 | tf_op jit(solution)/shard_map/all_gather | solution.py:243
  341.7 10.7 multiply_convert_fusion.1
  353.0 5.0 maximum_bitcast_fusion
  359.5 5.9 fusion.71
  370.9 253.1 %all-gather.4.cloned.1.call-done = bf16[512,512,2,2]{1,3,2,0:T(2,128)(2,1)} async-done(((bf16[4,512,2,2]{1,3,2,0:T(2,128)(2,1)}), bf16[512,512,2,2]{1,3,2,0:T(2,128)(2,1)}) %all-gather.4.cloned.1.call-update) | async-done | bytes 2097168 | tf_op jit(solution)/shard_map/all_gather | solution.py:252
  624.0 10.5 copy.100
  634.4 5.2 fusion.2
  639.7 4.1 fusion.4
  646.2 2.3 fusion.67
  651.2 1.3 fusion.21
  652.5 1.3 fusion.17
  654.0 1.7 fusion.40
  657.0 1.3 convolution_bitcast_fusion.1
  660.3 1.5 collective-permute-start.3
  661.8 3.4 collective-permute-done.3
  665.5 1.3 fusion.9
  666.8 1.3 fusion.8
  668.2 1.3 fusion.7
  669.5 6.9 fusion.72
  676.4 3.2 reshape.1188
  679.6 2.8 fusion.66
  685.8 657.9 %all-gather.6.cloned.1.call-done = bf16[512,512,2,2]{1,3,2,0:T(2,128)(2,1)} async-done(((bf16[4,512,2,2]{1,3,2,0:T(2,128)(2,1)}), bf16[512,512,2,2]{1,3,2,0:T(2,128)(2,1)}) %all-gather.6.cloned.1.call-update) | async-done | bytes 2097168 | tf_op jit(solution)/shard_map/all_gather | solution.py:252
  1343.6 10.5 copy.112
  1354.1 5.2 fusion.1
  1359.4 4.1 fusion.3
  1365.9 1.3 fusion.19
  1367.2 1.3 fusion.15
  1368.6 1.7 multiply_reduce_fusion
  1370.3 102.4 %all-reduce = (f32[4]{0:T(128)S(1)}, f32[4]{0:T(128)S(1)}) all-reduce(f32[4]{0:T(128)S(1)} %get-tuple-element.34, f32[4]{0:T(128)S(1)} %get-tuple-element.53), channel_id=1, replica_groups=mesh['box'=128,'exc'=4] {'exc'}, use_global_device_ids=true, to_apply=%region_3.4 | all-reduce | flops 8 | bytes 64 | tf_op jit(solution)/shard_map/psum | solution.py:258
  (110 shorter events, 29.9 us)
Async XLA Ops:
  7.2 616.8 %all-gather.4.cloned.1.call-start = ((), (), s32[]{:S(2)}) async-start(), calls=%async_computation | async-start | bytes 2113536 | tf_op jit(solution)/shard_map/all_gather | solution.py:252
  8.6 343.8 %copy-start.8 = (f32[2,2]{1,0:T(2,128)S(1)}, f32[2,2]{1,0:T(2,128)}, u32[]{:S(2)}) copy-start(f32[2,2]{1,0:T(2,128)} %constant.150) | copy-start | bytes 52
  8.7 349.6 %collective-permute-start = (bf16[2,2,4,512]{3,2,1,0:T(4,128)(2,1)S(1)}, bf16[2,2,4,512]{3,2,1,0:T(4,128)(2,1)S(1)}, u32[]{:S(2)}, u32[]{:S(2)}) collective-permute-start(bf16[2,2,4,512]{3,2,1,0:T(4,128)(2,1)S(1)} %multiply_convert_fusion.3), channel_id=1, source_target_pairs={{0,4},{4,8},{8,12},{12,16},{16,20},{20,24},{24,28},{28,32},{32,36}... | collective-permute-start | bytes 49160 | tf_op jit(solution)/shard_map/ppermute | solution.py:26
  13.5 344.8 %collective-permute-start.1 = (bf16[2,2,4,512]{3,2,1,0:T(4,128)(2,1)S(1)}, bf16[2,2,4,512]{3,2,1,0:T(4,128)(2,1)S(1)}, u32[]{:S(2)}, u32[]{:S(2)}) collective-permute-start(bf16[2,2,4,512]{3,2,1,0:T(4,128)(2,1)S(1)} %multiply_convert_fusion.3), channel_id=1, source_target_pairs={{4,0},{8,4},{12,8},{16,12},{20,16},{24,20},{28,24},{32,28},{36,32}... | collective-permute-start | bytes 49160 | tf_op jit(solution)/shard_map/ppermute | solution.py:29
  18.1 1325.6 %all-gather.6.cloned.1.call-start = ((), (), s32[]{:S(2)}) async-start(), calls=%async_computation.1 | async-start | bytes 2113536 | tf_op jit(solution)/shard_map/all_gather | solution.py:252
  352.9 5.6 copy-start.11
  352.9 5.6 copy-start.14
  353.0 5.9 copy-start.10
  353.0 5.9 copy-start.13
  353.0 6.2 copy-start.9
  353.0 6.2 copy-start.12
  365.5 3.3 copy-start.1
  366.4 1.3 copy-start.2
  366.4 3.4 copy-start
  634.4 5.2 copy-start.4
  634.4 5.3 copy-start.7
  659.0 2.8 collective-permute-start.2
  660.3 4.9 collective-permute-start.3
  679.6 3.0 copy-start.3
  1354.1 5.2 copy-start.5
  1354.1 5.3 copy-start.6
Sparse Core Ops, SparseCore 0:
  18.2 605.7 all-gather.3
  659.1 684.4 all-gather.5

commit v2 on v0

--- a/solution.py
+++ b/solution.py
@@ -243,17 +243,14 @@
     outputs = []
     for term_index in range(2):
         sources = (contrast_real[None, None] * fields.astype(jnp.float32)).astype(jnp.bfloat16)
+        encoded = encode(sources, enc_table)
+        translated = translate(
+            lax.all_to_all(encoded, "box", split_axis=0, concat_axis=3, tiled=True), translators
+        )
+        if term_index == 0:
+            sources, translated = lax.optimization_barrier((sources, translated))
         near_part = near_field(sources, box_pos)
-        encoded = encode(sources, enc_table)
-        returned = lax.all_to_all(
-            translate(
-                lax.all_to_all(encoded, "box", split_axis=0, concat_axis=3, tiled=True), translators
-            ),
-            "box",
-            split_axis=3,
-            concat_axis=0,
-            tiled=True,
-        )
+        returned = lax.all_to_all(translated, "box", split_axis=3, concat_axis=0, tiled=True)
         fields = (near_part + decode(returned, dec_table)).astype(jnp.bfloat16)
         outputs.append(fields)
     first_sq = jnp.sum(jnp.square(outputs[0].astype(jnp.float32)), axis=(0, 1, 3))

time: 216 us -> 194 us (0.90)
  waiting for transfers between devices: 28.8 us -> 15.6 us
  starting transfers between devices: 76 us -> 72.2 us
  local copies, waits for them, and re-layouts: 26.4 us -> 23.3 us
    all_to_all x2, waiting for transfers between devices: 28.8 us -> 15.5 us  [shards(): lax.all_to_all(translated, 'box', split_axis=3, concat_axis=0, tiled=True)]
    ppermute x2, starting transfers between devices: 9.43 us -> 4.66 us  [padded(): lax.ppermute(lax.slice_in_dim(block, block.shape[dim] - width, None, axis...]
    dot_general x12, matrix products: 14.9 us -> 12.1 us  [masked_flips(): jnp.dot(rows, jnp.asarray(matrix, rows.dtype), precision=precision, prefe...]
    all_to_all x2, starting transfers between devices: 28.6 us -> 31.1 us  [shards(): lax.all_to_all(translated, 'box', split_axis=3, concat_axis=0, tiled=True)]
  transfers between devices with their start and end apart: 8 -> 8, of which waited for: 2 -> 2; matrix products, arithmetic and copies ran while one was open for 30% -> 31% of each run, Pallas kernels for 0% -> 0%
where the time goes in v2:
time: 194 us; the launch traced here: 193 us
  starting transfers between devices  72.2 us (37%)
  matrix products  47.2 us (24%)
  local copies, waits for them, and re-layouts  23.3 us (12%)
  other arithmetic  20 us (10%)
  waiting for transfers between devices  15.6 us (8%)
  blocking collectives  13 us (7%)
    all_to_all x2, starting transfers between devices, shards(): lax.all_to_all(encoded, 'box', split_axis=0, concat_axis=3, tiled=True)  33.8 us
    all_to_all x2, starting transfers between devices, shards(): lax.all_to_all(translated, 'box', split_axis=3, concat_axis=0, tiled=True)  31.1 us
    all_to_all x2, waiting for transfers between devices, shards(): lax.all_to_all(translated, 'box', split_axis=3, concat_axis=0, tiled=True)  15.5 us
    psum x1, blocking collectives, shards(): first_sum, second_sum = lax.psum((first_sq, second_sq), 'exc')  13 us
    dot_general x2, matrix products, near_field(): lax.dot_general(pieces.reshape(8, -1, V), blocks, (((2,), (2,)), ((0,), (...  12.8 us
    dot_general x12, matrix products, masked_flips(): jnp.dot(rows, jnp.asarray(matrix, rows.dtype), precision=precision, prefe...  12.1 us
    slice x2, local copies, waits for them, and re-layouts, near_field(): product[:, 0, :, 0] - product[:, 1, :, 1]  5.38 us
    neg x1, other arithmetic, translator(): now_re, now_im = (jnp.zeros_like(inverse), -inverse)  5.38 us
  transfers between devices with their start and end apart: 8, of which 2 were waited for; matrix products, arithmetic and copies ran while one was open for 31% of the time, Pallas kernels for 0%

profile of v2, /device:TPU:1, one launch (start us, length us, event | category | flops | bytes accessed | tf_op | source)
XLA Modules:
  0.0 192.5 jit_solution(11340264002734008694)
XLA Ops:
  2.1 1.3 convolution_bitcast_fusion.2
  3.4 1.3 convolution_bitcast_fusion.3
  5.9 18.6 %all-to-all-start = ((bf16[512,2,2,4]{3,2,1,0:T(2,128)(2,1)}), bf16[512,2,2,4]{3,2,1,0:T(2,128)(2,1)S(1)}, u32[]{:S(2)}, u32[]{:S(2)}) async-start(bf16[512,2,2,4]{3,2,1,0:T(2,128)(2,1)} %copy.99), calls=%async_computation | async-start | bytes 1048576 | tf_op jit(solution)/shard_map/all_to_all | solution.py:248
  30.2 5.4 %fusion.33 = (f32[512,512]{1,0:T(8,128)S(1)}, f32[512,512]{1,0:T(8,128)S(1)}, f32[512,512]{1,0:T(8,128)S(1)}, f32[512,512]{1,0:T(8,128)S(1)}, f32[512,512]{1,0:T...) fusion(f32[512]{0:T(512)S(1)} %get-tuple-element.51, ...), kind=kLoop, calls=%fused_computation.83 | loop fusion | flops 10747904 | bytes 14686208 | tf_op jit(solution)/shard_map/vmap()/neg | solution.py:54
  35.6 5.0 %multiply_convert_fusion.1 = (bf16[1,4,512,512]{3,2,1,0:T(8,128)(2,1)S(1)}, bf16[1,4,512,512]{3,2,1,0:T(8,128)(2,1)S(1)}) fusion(f32[512,512]{1,0:T(8,128)S(1)} %get-tuple-element.42, f32[512,512]{1,0:T(8,128)S(1)} %get-tuple-element.43, f32[512,512]{1,0:T(8,128)S(1)} %get-tuple-element.41, f32[512,512]{1,0:T(8,128)S(1)} %get-tuple-element.36, ...), kind=kLoop, calls=%fused_computation.4 | loop fusion | flops 36700160 | bytes 18874416 | tf_op jit(solution)/shard_map/convert.6
  40.6 2.3 %maximum_bitcast_fusion = bf16[4,2,512,512]{3,2,0,1:T(8,128)(2,1)} fusion(bf16[1,4,512,512]{3,2,1,0:T(8,128)(2,1)S(1)} %get-tuple-element.10, bf16[1,4,512,512]{3,2,1,0:T(8,128)(2,1)S(1)} %get-tuple-element.9), kind=kLoop, calls=%fused_computation.2 | loop fusion | flops 2097152 | bytes 8388608 | tf_op jit(solution)/shard_map/vmap()/transpose | solution.py:96
  44.0 2.3 %fusion.2 = f32[4,2,2,512]{3,2,1,0:T(2,128)S(1)} fusion(bf16[4,2,2,512]{3,2,1,0:T(2,128)(2,1)S(1)} %all_to_all.55, bf16[4,2,512,512]{3,2,0,1:T(8,128)(2,1)} %maximum_bitcast_fusion), kind=kOutput, calls=%fused_computation.12 | convolution fusion | flops 8388608 | bytes 2146304 | tf_op jit(solution)/shard_map/kts,kxes->kxet/dot_general | solution.py:218
  46.3 2.3 %fusion.4 = f32[4,2,2,512]{3,2,1,0:T(2,128)S(1)} fusion(bf16[4,2,2,512]{3,2,1,0:T(2,128)(2,1)S(1)} %all_to_all.55, bf16[4,2,512,512]{3,2,0,1:T(8,128)(2,1)} %maximum_bitcast_fusion), kind=kOutput, calls=%fused_computation.14 | convolution fusion | flops 8388608 | bytes 2146304 | tf_op jit(solution)/shard_map/kts,kxes->kxet/dot_general | solution.py:221
  48.6 2.5 %collective-permute-start = (bf16[2,2,4,512]{3,2,1,0:T(4,128)(2,1)S(1)}, bf16[2,2,4,512]{3,2,1,0:T(4,128)(2,1)S(1)}, u32[]{:S(2)}, u32[]{:S(2)}) collective-permute-start(bf16[2,2,4,512]{3,2,1,0:T(4,128)(2,1)S(1)} %multiply_convert_fusion.3), channel_id=1, source_target_pairs={{0,4},{4,8},{8,12},{12,16},{16,20},{20,24},{24,28},{28,32},{32,36}... | collective-permute-start | bytes 49160 | tf_op jit(solution)/shard_map/ppermute | solution.py:26
  53.8 17.0 %all-to-all-start.1 = ((bf16[4,2,2,512]{0,2,1,3:T(2,128)(2,1)}), bf16[4,2,2,512]{0,2,1,3:T(2,128)(2,1)}, u32[]{:S(2)}, u32[]{:S(2)}) async-start(bf16[4,2,2,512]{0,2,1,3:T(2,128)(2,1)} %copy.107), calls=%async_computation.1 | async-start | bytes 1048576 | tf_op jit(solution)/shard_map/all_to_all | solution.py:253
  72.1 5.9 %fusion.67 = f32[8,32,1024]{2,1,0:T(8,128)S(1)} fusion(bf16[8,32,512]{2,1,0:T(8,128)(2,1)S(1)} %bitcast.179, bf16[8,1024,512]{2,1,0:T(8,128)(2,1)} %constant.138.clone), kind=kOutput, calls=%fused_computation.166 | convolution fusion | flops 268435456 | bytes 9699328 | tf_op jit(solution)/shard_map/dot_general | solution.py:181
  78.1 1.9 reshape.1232
  80.0 2.6 %fusion.66 = (f32[8,1,16,1,512]{4,3,2,1,0:T(1,128)S(1)}, f32[8,1,16,1,512]{4,3,2,1,0:T(1,128)S(1)}, f32[8,1,16,1,512]{4,3,2,1,0:T(1,128)S(1)}, f32[8,1,16,1,512]{4,3,2,1,0:T(1,128)S(1)}) fusion(f32[8,2,16,2,512]{4,3,2,1,0:T(2,128)} %reshape.1232), kind=kLoop, calls=%fused_computation.165 | loop fusion | bytes 2097152 | tf_op jit(solution)/shard_map/slice | solution.py:188
  85.9 1.9 all-to-all-done.1
  89.8 1.3 fusion.23
  92.7 1.7 fusion.47
  94.4 2.2 %collective-permute-start.2 = (bf16[2,2,4,512]{3,2,1,0:T(4,128)(2,1)S(1)}, bf16[2,2,4,512]{3,2,1,0:T(4,128)(2,1)S(1)}, u32[]{:S(2)}, u32[]{:S(2)}) collective-permute-start(bf16[2,2,4,512]{3,2,1,0:T(4,128)(2,1)S(1)} %get-tuple-element.32), channel_id=1, source_target_pairs={{0,4},{4,8},{8,12},{12,16},{16,20},{20,24},{24,28},{28,32},{32,36}... | collective-permute-start | bytes 49160 | tf_op jit(solution)/shard_map/ppermute | solution.py:26
  97.9 1.3 convolution_bitcast_fusion
  101.7 15.2 %all-to-all-start.2 = ((bf16[512,2,2,4]{3,2,1,0:T(2,128)(2,1)}), bf16[512,2,2,4]{3,2,1,0:T(2,128)(2,1)}, u32[]{:S(2)}, u32[]{:S(2)}) async-start(bf16[512,2,2,4]{3,2,1,0:T(2,128)(2,1)} %copy.115), calls=%async_computation.2 | async-start | bytes 1048576 | tf_op jit(solution)/shard_map/all_to_all | solution.py:248
  117.2 1.3 fusion.9
  118.5 1.3 fusion.8
  119.9 1.3 fusion.7
  121.2 6.9 %fusion.68 = f32[8,32,1024]{2,1,0:T(8,128)} fusion(bf16[8,32,512]{2,1,0:T(8,128)(2,1)S(1)} %bitcast.178, bf16[8,1024,512]{2,1,0:T(8,128)(2,1)} %constant.138.clone), kind=kOutput, calls=%fused_computation.167 | convolution fusion | flops 268435456 | bytes 9699328 | tf_op jit(solution)/shard_map/dot_general | solution.py:181
  128.2 3.1 %reshape.1236 = f32[8,2,16,2,512]{4,3,2,1,0:T(2,128)} reshape(f32[8,32,1024]{2,1,0:T(8,128)} %fusion.68) | data formatting | bytes 2097152 | tf_op jit(solution)/shard_map/reshape | solution.py:185
  131.2 2.8 %fusion.65 = (f32[8,1,16,1,512]{4,3,2,1,0:T(1,128)S(1)}, f32[8,1,16,1,512]{4,3,2,1,0:T(1,128)S(1)}, f32[8,1,16,1,512]{4,3,2,1,0:T(1,128)S(1)}, f32[8,1,16,1,512]{4,3,2,1,0:T(1,128)S(1)}) fusion(f32[8,2,16,2,512]{4,3,2,1,0:T(2,128)} %reshape.1236), kind=kLoop, calls=%fused_computation.164 | loop fusion | bytes 2097152 | tf_op jit(solution)/shard_map/slice | solution.py:188
  138.3 2.3 %fusion.1 = f32[4,2,2,512]{3,2,1,0:T(2,128)S(1)} fusion(bf16[4,2,2,512]{3,2,1,0:T(2,128)(2,1)S(1)} %all_to_all.63, bf16[4,2,512,512]{3,2,0,1:T(8,128)(2,1)} %maximum_bitcast_fusion), kind=kOutput, calls=%fused_computation.11 | convolution fusion | flops 8388608 | bytes 2146304 | tf_op jit(solution)/shard_map/kts,kxes->kxet/dot_general | solution.py:218
  140.5 2.3 %fusion.3 = f32[4,2,2,512]{3,2,1,0:T(2,128)S(1)} fusion(bf16[4,2,2,512]{3,2,1,0:T(2,128)(2,1)S(1)} %all_to_all.63, bf16[4,2,512,512]{3,2,0,1:T(8,128)(2,1)} %maximum_bitcast_fusion), kind=kOutput, calls=%fused_computation.13 | convolution fusion | flops 8388608 | bytes 2146304 | tf_op jit(solution)/shard_map/kts,kxes->kxet/dot_general | solution.py:221
  144.1 14.1 %all-to-all-start.3 = ((bf16[4,2,2,512]{0,2,1,3:T(2,128)(2,1)}), bf16[4,2,2,512]{0,2,1,3:T(2,128)(2,1)}, u32[]{:S(2)}, u32[]{:S(2)}) async-start(bf16[4,2,2,512]{0,2,1,3:T(2,128)(2,1)} %copy.118), calls=%async_computation.3 | async-start | bytes 1048576 | tf_op jit(solution)/shard_map/all_to_all | solution.py:253
  158.2 1.9 fusion.6
  160.1 13.6 %all-to-all-done.3 = bf16[4,2,2,512]{0,2,1,3:T(2,128)(2,1)} async-done(((bf16[4,2,2,512]{0,2,1,3:T(2,128)(2,1)}), bf16[4,2,2,512]{0,2,1,3:T(2,128)(2,1)}, u32[]{:S(2)}, u32[]{:S(2)}) %all-to-all-start.3) | async-done | bytes 16416 | tf_op jit(solution)/shard_map/all_to_all | solution.py:253
  176.3 2.7 %multiply_reduce_fusion = (f32[4]{0:T(128)S(1)}, bf16[2,2,4,512]{3,2,1,0:T(4,128)(2,1)}) fusion(f32[1,2,4,512]{3,2,1,0:T(4,128)S(1)} %get-tuple-element.20, f32[1,2,4,512]{3,2,1,0:T(4,128)S(1)} %get-tuple-element.19, f32[2,2,4,256]{2,3,1,0:T(8,128)S(1)} %bitcast.170, f32[256,512,1,1]{1,0,3,2:T(8,128)} %fusion.6), kind=kOutput, calls=%fused_computation.108 | convolution fusion | flops 25214972 | bytes 589840 | tf_op jit(solution)/shard_map/dot_general | solution.py:201
  179.0 13.0 %all-reduce = (f32[4]{0:T(128)S(1)}, f32[4]{0:T(128)S(1)}) all-reduce(f32[4]{0:T(128)S(1)} %get-tuple-element.31, f32[4]{0:T(128)S(1)} %get-tuple-element.53), channel_id=1, replica_groups=mesh['box'=128,'exc'=4] {'exc'}, use_global_device_ids=true, to_apply=%region_3.4 | all-reduce | flops 8 | bytes 64 | tf_op jit(solution)/shard_map/psum | solution.py:258
  (95 shorter events, 32.5 us)
Async XLA Ops:
  5.9 37.1 %all-to-all-start = ((bf16[512,2,2,4]{3,2,1,0:T(2,128)(2,1)}), bf16[512,2,2,4]{3,2,1,0:T(2,128)(2,1)S(1)}, u32[]{:S(2)}, u32[]{:S(2)}) async-start(bf16[512,2,2,4]{3,2,1,0:T(2,128)(2,1)} %copy.99), calls=%async_computation | async-start | bytes 1048576 | tf_op jit(solution)/shard_map/all_to_all | solution.py:248
  43.0 9.4 %copy-start.5 = (f32[2,2]{1,0:T(2,128)S(1)}, f32[2,2]{1,0:T(2,128)}, u32[]{:S(2)}) copy-start(f32[2,2]{1,0:T(2,128)} %constant.148) | copy-start | bytes 52
  43.0 28.2 %copy-start.8 = (pred[256]{0:T(512)(128)(4,1)S(1)}, pred[256]{0:T(512)(128)(4,1)}, u32[]{:S(2)}) copy-start(pred[256]{0:T(512)(128)(4,1)} %constant.152) | copy-start | bytes 772
  43.0 28.2 %copy-start.11 = (bf16[512,512]{1,0:T(8,128)(2,1)S(1)}, bf16[512,512]{1,0:T(8,128)(2,1)}, u32[]{:S(2)}) copy-start(bf16[512,512]{1,0:T(8,128)(2,1)} %constant.132.clone) | copy-start | bytes 1572868
  43.1 28.4 %copy-start.7 = (pred[256]{0:T(512)(128)(4,1)S(1)}, pred[256]{0:T(512)(128)(4,1)}, u32[]{:S(2)}) copy-start(pred[256]{0:T(512)(128)(4,1)} %constant.151) | copy-start | bytes 772
  43.1 28.4 %copy-start.10 = (bf16[512,512]{1,0:T(8,128)(2,1)S(1)}, bf16[512,512]{1,0:T(8,128)(2,1)}, u32[]{:S(2)}) copy-start(bf16[512,512]{1,0:T(8,128)(2,1)} %constant.134.clone) | copy-start | bytes 1572868
  44.0 27.9 %copy-start.6 = (pred[256]{0:T(512)(128)(4,1)S(1)}, pred[256]{0:T(512)(128)(4,1)}, u32[]{:S(2)}) copy-start(pred[256]{0:T(512)(128)(4,1)} %constant.150) | copy-start | bytes 772
  44.0 27.9 %copy-start.9 = (bf16[512,512]{1,0:T(8,128)(2,1)S(1)}, bf16[512,512]{1,0:T(8,128)(2,1)}, u32[]{:S(2)}) copy-start(bf16[512,512]{1,0:T(8,128)(2,1)} %constant.136.clone) | copy-start | bytes 1572868
  48.6 22.2 %collective-permute-start = (bf16[2,2,4,512]{3,2,1,0:T(4,128)(2,1)S(1)}, bf16[2,2,4,512]{3,2,1,0:T(4,128)(2,1)S(1)}, u32[]{:S(2)}, u32[]{:S(2)}) collective-permute-start(bf16[2,2,4,512]{3,2,1,0:T(4,128)(2,1)S(1)} %multiply_convert_fusion.3), channel_id=1, source_target_pairs={{0,4},{4,8},{8,12},{12,16},{16,20},{20,24},{24,28},{28,32},{32,36}... | collective-permute-start | bytes 49160 | tf_op jit(solution)/shard_map/ppermute | solution.py:26
  51.1 19.8 %collective-permute-start.1 = (bf16[2,2,4,512]{3,2,1,0:T(4,128)(2,1)S(1)}, bf16[2,2,4,512]{3,2,1,0:T(4,128)(2,1)S(1)}, u32[]{:S(2)}, u32[]{:S(2)}) collective-permute-start(bf16[2,2,4,512]{3,2,1,0:T(4,128)(2,1)S(1)} %multiply_convert_fusion.3), channel_id=1, source_target_pairs={{4,0},{8,4},{12,8},{16,12},{20,16},{24,20},{28,24},{32,28},{36,32}... | collective-permute-start | bytes 49160 | tf_op jit(solution)/shard_map/ppermute | solution.py:29
  53.8 34.0 %all-to-all-start.1 = ((bf16[4,2,2,512]{0,2,1,3:T(2,128)(2,1)}), bf16[4,2,2,512]{0,2,1,3:T(2,128)(2,1)}, u32[]{:S(2)}, u32[]{:S(2)}) async-start(bf16[4,2,2,512]{0,2,1,3:T(2,128)(2,1)} %copy.107), calls=%async_computation.1 | async-start | bytes 1048576 | tf_op jit(solution)/shard_map/all_to_all | solution.py:253
  78.1 5.8 %copy-start.1 = (f32[512,512]{1,0:T(8,128)S(1)}, f32[512,512]{1,0:T(8,128)}, u32[]{:S(2)}) copy-start(f32[512,512]{1,0:T(8,128)} %constant.140.clone) | copy-start | bytes 3145732
  80.0 2.8 %copy-start.2 = (f32[512,512]{1,0:T(8,128)S(1)}, f32[512,512]{1,0:T(8,128)}, u32[]{:S(2)}) copy-start(f32[512,512]{1,0:T(8,128)} %constant.139.clone) | copy-start | bytes 3145732
  80.0 4.9 %copy-start = (f32[512,512]{1,0:T(8,128)S(1)}, f32[512,512]{1,0:T(8,128)}, u32[]{:S(2)}) copy-start(f32[512,512]{1,0:T(8,128)} %constant.141.clone) | copy-start | bytes 3145732
  94.4 22.5 %collective-permute-start.2 = (bf16[2,2,4,512]{3,2,1,0:T(4,128)(2,1)S(1)}, bf16[2,2,4,512]{3,2,1,0:T(4,128)(2,1)S(1)}, u32[]{:S(2)}, u32[]{:S(2)}) collective-permute-start(bf16[2,2,4,512]{3,2,1,0:T(4,128)(2,1)S(1)} %get-tuple-element.32), channel_id=1, source_target_pairs={{0,4},{4,8},{8,12},{12,16},{16,20},{20,24},{24,28},{28,32},{32,36}... | collective-permute-start | bytes 49160 | tf_op jit(solution)/shard_map/ppermute | solution.py:26
  96.6 20.3 %collective-permute-start.3 = (bf16[2,2,4,512]{3,2,1,0:T(4,128)(2,1)S(1)}, bf16[2,2,4,512]{3,2,1,0:T(4,128)(2,1)S(1)}, u32[]{:S(2)}, u32[]{:S(2)}) collective-permute-start(bf16[2,2,4,512]{3,2,1,0:T(4,128)(2,1)S(1)} %get-tuple-element.32), channel_id=1, source_target_pairs={{4,0},{8,4},{12,8},{16,12},{20,16},{24,20},{28,24},{32,28},{36,32}... | collective-permute-start | bytes 49160 | tf_op jit(solution)/shard_map/ppermute | solution.py:29
  101.7 34.6 %all-to-all-start.2 = ((bf16[512,2,2,4]{3,2,1,0:T(2,128)(2,1)}), bf16[512,2,2,4]{3,2,1,0:T(2,128)(2,1)}, u32[]{:S(2)}, u32[]{:S(2)}) async-start(bf16[512,2,2,4]{3,2,1,0:T(2,128)(2,1)} %copy.115), calls=%async_computation.2 | async-start | bytes 1048576 | tf_op jit(solution)/shard_map/all_to_all | solution.py:248
  131.2 2.9 %copy-start.3 = (f32[512,512]{1,0:T(8,128)S(1)}, f32[512,512]{1,0:T(8,128)}, u32[]{:S(2)}) copy-start(f32[512,512]{1,0:T(8,128)} %constant.139.clone) | copy-start | bytes 3145732
  140.5 35.2 %copy-start.4 = (bf16[2,512,512]{2,1,0:T(8,128)(2,1)S(1)}, bf16[2,512,512]{2,1,0:T(8,128)(2,1)}, u32[]{:S(2)}) copy-start(bf16[2,512,512]{2,1,0:T(8,128)(2,1)} %param.53) | copy-start | bytes 3145732
  144.1 29.6 %all-to-all-start.3 = ((bf16[4,2,2,512]{0,2,1,3:T(2,128)(2,1)}), bf16[4,2,2,512]{0,2,1,3:T(2,128)(2,1)}, u32[]{:S(2)}, u32[]{:S(2)}) async-start(bf16[4,2,2,512]{0,2,1,3:T(2,128)(2,1)} %copy.118), calls=%async_computation.3 | async-start | bytes 1048576 | tf_op jit(solution)/shard_map/all_to_all | solution.py:253

commit v3 on v2

--- a/solution.py
+++ b/solution.py
@@ -247,8 +247,7 @@
         translated = translate(
             lax.all_to_all(encoded, "box", split_axis=0, concat_axis=3, tiled=True), translators
         )
-        if term_index == 0:
-            sources, translated = lax.optimization_barrier((sources, translated))
+        sources, translated = lax.optimization_barrier((sources, translated))
         near_part = near_field(sources, box_pos)
         returned = lax.all_to_all(translated, "box", split_axis=3, concat_axis=0, tiled=True)
         fields = (near_part + decode(returned, dec_table)).astype(jnp.bfloat16)

time: 194 us -> 187 us (0.964)
  blocking collectives: 13 us -> 39.6 us
  starting transfers between devices: 72.2 us -> 54.3 us
  waiting for transfers between devices: 15.6 us -> 3.61 us
  local copies, waits for them, and re-layouts: 23.3 us -> 19.8 us
    all_to_all x0 -> x1, blocking collectives: none -> 27 us  [shards(): lax.all_to_all(encoded, 'box', split_axis=0, concat_axis=3, tiled=True)]
    all_to_all x2 -> x1, starting transfers between devices: 33.8 us -> 18.6 us  [shards(): lax.all_to_all(encoded, 'box', split_axis=0, concat_axis=3, tiled=True)]
    all_to_all x2, waiting for transfers between devices: 15.5 us -> 3.6 us  [shards(): lax.all_to_all(translated, 'box', split_axis=3, concat_axis=0, tiled=True)]
    all_to_all x2, starting transfers between devices: 31.1 us -> 28.4 us  [shards(): lax.all_to_all(translated, 'box', split_axis=3, concat_axis=0, tiled=True)]
  transfers between devices with their start and end apart: 8 -> 7, of which waited for: 2 -> 1; matrix products, arithmetic and copies ran while one was open for 31% -> 29% of each run, Pallas kernels for 0% -> 0%
where the time goes in v3:
time: 187 us; the launch traced here: 186 us
  starting transfers between devices  54.3 us (29%)
  matrix products  47.1 us (25%)
  blocking collectives  39.6 us (21%)
  other arithmetic  20 us (11%)
  local copies, waits for them, and re-layouts  19.8 us (11%)
  waiting for transfers between devices  3.61 us (2%)
    all_to_all x2, starting transfers between devices, shards(): lax.all_to_all(translated, 'box', split_axis=3, concat_axis=0, tiled=True)  28.4 us
    all_to_all x1, blocking collectives, shards(): lax.all_to_all(encoded, 'box', split_axis=0, concat_axis=3, tiled=True)  27 us
    all_to_all x1, starting transfers between devices, shards(): lax.all_to_all(encoded, 'box', split_axis=0, concat_axis=3, tiled=True)  18.6 us
    dot_general x2, matrix products, near_field(): lax.dot_general(pieces.reshape(8, -1, V), blocks, (((2,), (2,)), ((0,), (...  12.8 us
    psum x1, blocking collectives, shards(): first_sum, second_sum = lax.psum((first_sq, second_sq), 'exc')  12.6 us
    dot_general x12, matrix products, masked_flips(): jnp.dot(rows, jnp.asarray(matrix, rows.dtype), precision=precision, prefe...  12.1 us
    neg x1, other arithmetic, translator(): now_re, now_im = (jnp.zeros_like(inverse), -inverse)  5.38 us
    another operation x5, other arithmetic  5.09 us
  transfers between devices with their start and end apart: 7, of which 1 were waited for; matrix products, arithmetic and copies ran while one was open for 29% of the time, Pallas kernels for 0%

profile of v3, /device:TPU:1, one launch (start us, length us, event | category | flops | bytes accessed | tf_op | source)
XLA Modules:
  0.0 185.8 jit_solution(3300081614176316749)
XLA Ops:
  2.1 1.3 convolution_bitcast_fusion.2
  3.4 1.3 convolution_bitcast_fusion.3
  5.9 18.6 %all-to-all-start = ((bf16[512,2,2,4]{3,2,1,0:T(2,128)(2,1)}), bf16[512,2,2,4]{3,2,1,0:T(2,128)(2,1)S(1)}, u32[]{:S(2)}, u32[]{:S(2)}) async-start(bf16[512,2,2,4]{3,2,1,0:T(2,128)(2,1)} %copy.99), calls=%async_computation | async-start | bytes 1048576 | tf_op jit(solution)/shard_map/all_to_all | solution.py:248
  30.2 5.4 %fusion.33 = (f32[512,512]{1,0:T(8,128)S(1)}, f32[512,512]{1,0:T(8,128)S(1)}, f32[512,512]{1,0:T(8,128)S(1)}, f32[512,512]{1,0:T(8,128)S(1)}, f32[512,512]{1,0:T...) fusion(f32[512]{0:T(512)S(1)} %get-tuple-element.55, ...), kind=kLoop, calls=%fused_computation.83 | loop fusion | flops 10747904 | bytes 14686208 | tf_op jit(solution)/shard_map/vmap()/neg | solution.py:54
  35.6 5.0 %multiply_convert_fusion.1 = (bf16[1,4,512,512]{3,2,1,0:T(8,128)(2,1)S(1)}, bf16[1,4,512,512]{3,2,1,0:T(8,128)(2,1)S(1)}) fusion(f32[512,512]{1,0:T(8,128)S(1)} %get-tuple-element.46, f32[512,512]{1,0:T(8,128)S(1)} %get-tuple-element.47, f32[512,512]{1,0:T(8,128)S(1)} %get-tuple-element.45, f32[512,512]{1,0:T(8,128)S(1)} %get-tuple-element.40, ...), kind=kLoop, calls=%fused_computation.4 | loop fusion | flops 36700160 | bytes 18874416 | tf_op jit(solution)/shard_map/convert.6
  40.6 2.3 %maximum_bitcast_fusion = bf16[4,2,512,512]{3,2,0,1:T(8,128)(2,1)} fusion(bf16[1,4,512,512]{3,2,1,0:T(8,128)(2,1)S(1)} %get-tuple-element.14, bf16[1,4,512,512]{3,2,1,0:T(8,128)(2,1)S(1)} %get-tuple-element.13), kind=kLoop, calls=%fused_computation.2 | loop fusion | flops 2097152 | bytes 8388608 | tf_op jit(solution)/shard_map/vmap()/transpose | solution.py:96
  44.0 2.3 %fusion.2 = f32[4,2,2,512]{3,2,1,0:T(2,128)S(1)} fusion(bf16[4,2,2,512]{3,2,1,0:T(2,128)(2,1)S(1)} %all_to_all.55, bf16[4,2,512,512]{3,2,0,1:T(8,128)(2,1)} %maximum_bitcast_fusion), kind=kOutput, calls=%fused_computation.12 | convolution fusion | flops 8388608 | bytes 2146304 | tf_op jit(solution)/shard_map/kts,kxes->kxet/dot_general | solution.py:218
  46.3 2.3 %fusion.4 = f32[4,2,2,512]{3,2,1,0:T(2,128)S(1)} fusion(bf16[4,2,2,512]{3,2,1,0:T(2,128)(2,1)S(1)} %all_to_all.55, bf16[4,2,512,512]{3,2,0,1:T(8,128)(2,1)} %maximum_bitcast_fusion), kind=kOutput, calls=%fused_computation.14 | convolution fusion | flops 8388608 | bytes 2146304 | tf_op jit(solution)/shard_map/kts,kxes->kxet/dot_general | solution.py:221
  48.6 2.5 %collective-permute-start = (bf16[2,2,4,512]{3,2,1,0:T(4,128)(2,1)S(1)}, bf16[2,2,4,512]{3,2,1,0:T(4,128)(2,1)S(1)}, u32[]{:S(2)}, u32[]{:S(2)}) collective-permute-start(bf16[2,2,4,512]{3,2,1,0:T(4,128)(2,1)S(1)} %multiply_convert_fusion.3), channel_id=1, source_target_pairs={{0,4},{4,8},{8,12},{12,16},{16,20},{20,24},{24,28},{28,32},{32,36}... | collective-permute-start | bytes 49160 | tf_op jit(solution)/shard_map/ppermute | solution.py:26
  53.8 17.0 %all-to-all-start.1 = ((bf16[4,2,2,512]{0,2,1,3:T(2,128)(2,1)}), bf16[4,2,2,512]{0,2,1,3:T(2,128)(2,1)}, u32[]{:S(2)}, u32[]{:S(2)}) async-start(bf16[4,2,2,512]{0,2,1,3:T(2,128)(2,1)} %copy.107), calls=%async_computation.1 | async-start | bytes 1048576 | tf_op jit(solution)/shard_map/all_to_all | solution.py:252
  72.1 5.9 %fusion.67 = f32[8,32,1024]{2,1,0:T(8,128)S(1)} fusion(bf16[8,32,512]{2,1,0:T(8,128)(2,1)S(1)} %bitcast.181, bf16[8,1024,512]{2,1,0:T(8,128)(2,1)} %constant.138.clone), kind=kOutput, calls=%fused_computation.166 | convolution fusion | flops 268435456 | bytes 9699328 | tf_op jit(solution)/shard_map/dot_general | solution.py:181
  82.4 1.9 %fusion.5 = f32[256,512,1,1]{1,0,3,2:T(8,128)} fusion(f32[256,512]{1,0:T(8,128)S(1)} %convolution_select_fusion.4, f32[512,512]{1,0:T(8,128)S(1)} %copy-done, pred[256]{0:T(512)(128)(4,1)S(1)} %copy-done.6), kind=kOutput, calls=%fused_computation.22 | convolution fusion | flops 805437440 | bytes 2097408 | tf_op jit(solution)/shard_map/dot_general | solution.py:146
  84.3 3.6 %all-to-all-done.1 = bf16[4,2,2,512]{0,2,1,3:T(2,128)(2,1)} async-done(((bf16[4,2,2,512]{0,2,1,3:T(2,128)(2,1)}), bf16[4,2,2,512]{0,2,1,3:T(2,128)(2,1)}, u32[]{:S(2)}, u32[]{:S(2)}) %all-to-all-start.1) | async-done | bytes 16416 | tf_op jit(solution)/shard_map/all_to_all | solution.py:252
  87.9 2.0 %copy.169 = bf16[4,2,2,128,4]{0,3,4,2,1:T(8,128)(2,1)} copy(bf16[4,2,2,128,4]{0,2,1,4,3:T(2,128)(2,1)} %bitcast.30) | data formatting | bytes 32768 | tf_op jit(solution)/shard_map/all_to_all | solution.py:252
  89.9 1.8 all_to_all.59
  92.4 2.7 %fusion.47 = (f32[4]{0:T(128)S(1)}, bf16[2,2,4,512]{3,2,1,0:T(4,128)(2,1)S(1)}, bf16[2,2,4,512]{3,2,1,0:T(4,128)(2,1)}) fusion(f32[4,512]{1,0:T(4,128)S(1)} %convert_multiply_fusion.2, f32[1,2,4,512]{3,2,1,0:T(4,128)S(1)} %get-tuple-element.30, f32[1,2,4,512]{3,2,1,0:T(4,128)S(1)} %get-tuple-element.29, f32[2,2,4,256]{2,3,1,0:T(8,128)S(1)} %bitcast.169, ...), kind=kOutput, calls=%fused_computation.107 | convolution fusion | flops 25231356 | bytes 614416 | tf_op jit(solution)/shard_map/dot_general | solution.py:201
  96.5 1.3 convolution_bitcast_fusion.1
  98.3 27.0 %all_to_all.72 = bf16[512,2,2,4]{3,2,1,0:T(2,128)(2,1)S(1)} all-to-all(bf16[512,2,2,4]{3,2,1,0:T(2,128)(2,1)S(1)} %copy.110), channel_id=1, replica_groups=mesh['box'=128,'exc'=4] {'box'}, dimensions={0} | all-to-all | bytes 32768 | tf_op jit(solution)/shard_map/all_to_all | solution.py:248
  126.3 2.3 %fusion.1 = f32[4,2,2,512]{3,2,1,0:T(2,128)S(1)} fusion(bf16[4,2,2,512]{3,2,1,0:T(2,128)(2,1)S(1)} %all_to_all.63, bf16[4,2,512,512]{3,2,0,1:T(8,128)(2,1)} %maximum_bitcast_fusion), kind=kOutput, calls=%fused_computation.11 | convolution fusion | flops 8388608 | bytes 2146304 | tf_op jit(solution)/shard_map/kts,kxes->kxet/dot_general | solution.py:218
  128.5 2.3 %fusion.3 = f32[4,2,2,512]{3,2,1,0:T(2,128)S(1)} fusion(bf16[4,2,2,512]{3,2,1,0:T(2,128)(2,1)S(1)} %all_to_all.63, bf16[4,2,512,512]{3,2,0,1:T(8,128)(2,1)} %maximum_bitcast_fusion), kind=kOutput, calls=%fused_computation.13 | convolution fusion | flops 8388608 | bytes 2146304 | tf_op jit(solution)/shard_map/kts,kxes->kxet/dot_general | solution.py:221
  130.9 2.2 %collective-permute-start.2 = (bf16[2,2,4,512]{3,2,1,0:T(4,128)(2,1)S(1)}, bf16[2,2,4,512]{3,2,1,0:T(4,128)(2,1)S(1)}, u32[]{:S(2)}, u32[]{:S(2)}) collective-permute-start(bf16[2,2,4,512]{3,2,1,0:T(4,128)(2,1)S(1)} %get-tuple-element.9), channel_id=1, source_target_pairs={{0,4},{4,8},{8,12},{12,16},{16,20},{20,24},{24,28},{28,32},{32,36}... | collective-permute-start | bytes 49160 | tf_op jit(solution)/shard_map/ppermute | solution.py:26
  135.5 11.4 %all-to-all-start.3 = ((bf16[4,2,2,512]{0,2,1,3:T(2,128)(2,1)}), bf16[4,2,2,512]{0,2,1,3:T(2,128)(2,1)S(1)}, u32[]{:S(2)}, u32[]{:S(2)}) async-start(bf16[4,2,2,512]{0,2,1,3:T(2,128)(2,1)} %copy.118), calls=%async_computation.3 | async-start | bytes 1048576 | tf_op jit(solution)/shard_map/all_to_all | solution.py:252
  147.2 1.3 fusion.9
  148.6 1.3 fusion.8
  149.9 1.3 fusion.7
  151.3 6.9 %fusion.68 = f32[8,32,1024]{2,1,0:T(8,128)} fusion(bf16[8,32,512]{2,1,0:T(8,128)(2,1)S(1)} %bitcast.180, bf16[8,1024,512]{2,1,0:T(8,128)(2,1)} %constant.138.clone), kind=kOutput, calls=%fused_computation.167 | convolution fusion | flops 268435456 | bytes 9699328 | tf_op jit(solution)/shard_map/dot_general | solution.py:181
  158.2 3.1 %reshape.1236 = f32[8,2,16,2,512]{4,3,2,1,0:T(2,128)} reshape(f32[8,32,1024]{2,1,0:T(8,128)} %fusion.68) | data formatting | bytes 2097152 | tf_op jit(solution)/shard_map/reshape | solution.py:185
  161.3 2.8 %fusion.65 = (f32[8,1,16,1,512]{4,3,2,1,0:T(1,128)S(1)}, f32[8,1,16,1,512]{4,3,2,1,0:T(1,128)S(1)}, f32[8,1,16,1,512]{4,3,2,1,0:T(1,128)S(1)}, f32[8,1,16,1,512]{4,3,2,1,0:T(1,128)S(1)}) fusion(f32[8,2,16,2,512]{4,3,2,1,0:T(2,128)} %reshape.1236), kind=kLoop, calls=%fused_computation.164 | loop fusion | bytes 2097152 | tf_op jit(solution)/shard_map/slice | solution.py:188
  168.3 1.3 fusion.21
  169.6 1.3 fusion.25
  171.0 1.7 multiply_reduce_fusion
  172.7 12.6 %all-reduce = (f32[4]{0:T(128)S(1)}, f32[4]{0:T(128)S(1)}) all-reduce(f32[4]{0:T(128)S(1)} %get-tuple-element.35, f32[4]{0:T(128)S(1)} %get-tuple-element.57), channel_id=1, replica_groups=mesh['box'=128,'exc'=4] {'exc'}, use_global_device_ids=true, to_apply=%region_3.4 | all-reduce | flops 8 | bytes 64 | tf_op jit(solution)/shard_map/psum | solution.py:257
  (94 shorter events, 28.4 us)
Async XLA Ops:
  5.9 37.1 %all-to-all-start = ((bf16[512,2,2,4]{3,2,1,0:T(2,128)(2,1)}), bf16[512,2,2,4]{3,2,1,0:T(2,128)(2,1)S(1)}, u32[]{:S(2)}, u32[]{:S(2)}) async-start(bf16[512,2,2,4]{3,2,1,0:T(2,128)(2,1)} %copy.99), calls=%async_computation | async-start | bytes 1048576 | tf_op jit(solution)/shard_map/all_to_all | solution.py:248
  43.0 9.4 %copy-start.5 = (f32[2,2]{1,0:T(2,128)S(1)}, f32[2,2]{1,0:T(2,128)}, u32[]{:S(2)}) copy-start(f32[2,2]{1,0:T(2,128)} %constant.148) | copy-start | bytes 52
  43.0 28.2 %copy-start.8 = (pred[256]{0:T(512)(128)(4,1)S(1)}, pred[256]{0:T(512)(128)(4,1)}, u32[]{:S(2)}) copy-start(pred[256]{0:T(512)(128)(4,1)} %constant.152) | copy-start | bytes 772
  43.0 28.2 %copy-start.11 = (bf16[512,512]{1,0:T(8,128)(2,1)S(1)}, bf16[512,512]{1,0:T(8,128)(2,1)}, u32[]{:S(2)}) copy-start(bf16[512,512]{1,0:T(8,128)(2,1)} %constant.132.clone) | copy-start | bytes 1572868
  43.1 28.4 %copy-start.7 = (pred[256]{0:T(512)(128)(4,1)S(1)}, pred[256]{0:T(512)(128)(4,1)}, u32[]{:S(2)}) copy-start(pred[256]{0:T(512)(128)(4,1)} %constant.151) | copy-start | bytes 772
  43.1 28.4 %copy-start.10 = (bf16[512,512]{1,0:T(8,128)(2,1)S(1)}, bf16[512,512]{1,0:T(8,128)(2,1)}, u32[]{:S(2)}) copy-start(bf16[512,512]{1,0:T(8,128)(2,1)} %constant.134.clone) | copy-start | bytes 1572868
  43.9 27.9 %copy-start.6 = (pred[256]{0:T(512)(128)(4,1)S(1)}, pred[256]{0:T(512)(128)(4,1)}, u32[]{:S(2)}) copy-start(pred[256]{0:T(512)(128)(4,1)} %constant.150) | copy-start | bytes 772
  43.9 27.9 %copy-start.9 = (bf16[512,512]{1,0:T(8,128)(2,1)S(1)}, bf16[512,512]{1,0:T(8,128)(2,1)}, u32[]{:S(2)}) copy-start(bf16[512,512]{1,0:T(8,128)(2,1)} %constant.136.clone) | copy-start | bytes 1572868
  48.6 22.3 %collective-permute-start = (bf16[2,2,4,512]{3,2,1,0:T(4,128)(2,1)S(1)}, bf16[2,2,4,512]{3,2,1,0:T(4,128)(2,1)S(1)}, u32[]{:S(2)}, u32[]{:S(2)}) collective-permute-start(bf16[2,2,4,512]{3,2,1,0:T(4,128)(2,1)S(1)} %multiply_convert_fusion.3), channel_id=1, source_target_pairs={{0,4},{4,8},{8,12},{12,16},{16,20},{20,24},{24,28},{28,32},{32,36}... | collective-permute-start | bytes 49160 | tf_op jit(solution)/shard_map/ppermute | solution.py:26
  51.1 19.8 %collective-permute-start.1 = (bf16[2,2,4,512]{3,2,1,0:T(4,128)(2,1)S(1)}, bf16[2,2,4,512]{3,2,1,0:T(4,128)(2,1)S(1)}, u32[]{:S(2)}, u32[]{:S(2)}) collective-permute-start(bf16[2,2,4,512]{3,2,1,0:T(4,128)(2,1)S(1)} %multiply_convert_fusion.3), channel_id=1, source_target_pairs={{4,0},{8,4},{12,8},{16,12},{20,16},{24,20},{28,24},{32,28},{36,32}... | collective-permute-start | bytes 49160 | tf_op jit(solution)/shard_map/ppermute | solution.py:29
  53.8 34.0 %all-to-all-start.1 = ((bf16[4,2,2,512]{0,2,1,3:T(2,128)(2,1)}), bf16[4,2,2,512]{0,2,1,3:T(2,128)(2,1)}, u32[]{:S(2)}, u32[]{:S(2)}) async-start(bf16[4,2,2,512]{0,2,1,3:T(2,128)(2,1)} %copy.107), calls=%async_computation.1 | async-start | bytes 1048576 | tf_op jit(solution)/shard_map/all_to_all | solution.py:252
  78.0 3.3 %copy-start.1 = (f32[512,512]{1,0:T(8,128)S(1)}, f32[512,512]{1,0:T(8,128)}, u32[]{:S(2)}) copy-start(f32[512,512]{1,0:T(8,128)} %constant.140.clone) | copy-start | bytes 3145732
  79.0 1.3 copy-start.2
  79.0 3.4 %copy-start = (f32[512,512]{1,0:T(8,128)S(1)}, f32[512,512]{1,0:T(8,128)}, u32[]{:S(2)}) copy-start(f32[512,512]{1,0:T(8,128)} %constant.141.clone) | copy-start | bytes 3145732
  80.2 11.4 %copy-start.4 = (bf16[2,512,512]{2,1,0:T(8,128)(2,1)S(1)}, bf16[2,512,512]{2,1,0:T(8,128)(2,1)}, u32[]{:S(2)}) copy-start(bf16[2,512,512]{2,1,0:T(8,128)(2,1)} %param.53) | copy-start | bytes 3145732
  130.9 16.1 %collective-permute-start.2 = (bf16[2,2,4,512]{3,2,1,0:T(4,128)(2,1)S(1)}, bf16[2,2,4,512]{3,2,1,0:T(4,128)(2,1)S(1)}, u32[]{:S(2)}, u32[]{:S(2)}) collective-permute-start(bf16[2,2,4,512]{3,2,1,0:T(4,128)(2,1)S(1)} %get-tuple-element.9), channel_id=1, source_target_pairs={{0,4},{4,8},{8,12},{12,16},{16,20},{20,24},{24,28},{28,32},{32,36}... | collective-permute-start | bytes 49160 | tf_op jit(solution)/shard_map/ppermute | solution.py:26
  133.1 13.9 %collective-permute-start.3 = (bf16[2,2,4,512]{3,2,1,0:T(4,128)(2,1)S(1)}, bf16[2,2,4,512]{3,2,1,0:T(4,128)(2,1)S(1)}, u32[]{:S(2)}, u32[]{:S(2)}) collective-permute-start(bf16[2,2,4,512]{3,2,1,0:T(4,128)(2,1)S(1)} %get-tuple-element.9), channel_id=1, source_target_pairs={{4,0},{8,4},{12,8},{16,12},{20,16},{24,20},{28,24},{32,28},{36,32}... | collective-permute-start | bytes 49160 | tf_op jit(solution)/shard_map/ppermute | solution.py:29
  135.5 31.9 %all-to-all-start.3 = ((bf16[4,2,2,512]{0,2,1,3:T(2,128)(2,1)}), bf16[4,2,2,512]{0,2,1,3:T(2,128)(2,1)S(1)}, u32[]{:S(2)}, u32[]{:S(2)}) async-start(bf16[4,2,2,512]{0,2,1,3:T(2,128)(2,1)} %copy.118), calls=%async_computation.3 | async-start | bytes 1048576 | tf_op jit(solution)/shard_map/all_to_all | solution.py:252
  161.3 2.9 %copy-start.3 = (f32[512,512]{1,0:T(8,128)S(1)}, f32[512,512]{1,0:T(8,128)}, u32[]{:S(2)}) copy-start(f32[512,512]{1,0:T(8,128)} %constant.139.clone) | copy-start | bytes 3145732

commit v4 on v3

--- a/solution.py
+++ b/solution.py
@@ -215,14 +215,11 @@
 
 
 def translate(encoded, translators):
-    real_prod = jnp.einsum(
-        "kts,kxes->kxet", translators[:, 0], encoded, preferred_element_type=jnp.float32
-    )
-    imag_prod = jnp.einsum(
-        "kts,kxes->kxet", translators[:, 1], encoded, preferred_element_type=jnp.float32
+    product = jnp.einsum(
+        "kcts,kxes->kcxet", translators, encoded, preferred_element_type=jnp.float32
     )
     return jnp.stack(
-        [real_prod[:, 0] - imag_prod[:, 1], imag_prod[:, 0] + real_prod[:, 1]], axis=1
+        [product[:, 0, 0] - product[:, 1, 1], product[:, 1, 0] + product[:, 0, 1]], axis=1
     ).astype(jnp.bfloat16)
 
 

time: 187 us -> 184 us (0.984)
  other arithmetic: 20 us -> 17.9 us
  blocking collectives: 39.6 us -> 41.7 us
    dot_general x4 -> x2, matrix products: 9.1 us -> 6.3 us  [translate(): jnp.einsum('kcts,kxes->kcxet', translators, encoded, preferred_element_ty...]
    transpose x1 -> x0, other arithmetic: 2.31 us -> none  [build_translators(): return jax.vmap(one_direction)(jnp.transpose(dir_block))]
    dot_general x12, matrix products: 12.1 us -> 14.1 us  [masked_flips(): jnp.dot(rows, jnp.asarray(matrix, rows.dtype), precision=precision, prefe...]
    all_to_all x2, waiting for transfers between devices: 3.6 us -> 1.55 us  [shards(): lax.all_to_all(translated, 'box', split_axis=3, concat_axis=0, tiled=True)]
    all_to_all x1, blocking collectives: 27 us -> 29.1 us  [shards(): lax.all_to_all(encoded, 'box', split_axis=0, concat_axis=3, tiled=True)]
    another operation x7 -> x5, other arithmetic: 5.14 us -> 5.9 us
  transfers between devices with their start and end apart: 7 -> 7, of which waited for: 1 -> 2; matrix products, arithmetic and copies ran while one was open for 29% -> 30% of each run, Pallas kernels for 0% -> 0%
where the time goes in v4:
time: 184 us; the launch traced here: 183 us
  starting transfers between devices  52.8 us (29%)
  matrix products  46.4 us (25%)
  blocking collectives  41.7 us (23%)
  local copies, waits for them, and re-layouts  19.8 us (11%)
  other arithmetic  17.9 us (10%)
  waiting for transfers between devices  2.99 us (2%)
    all_to_all x1, blocking collectives, shards(): lax.all_to_all(encoded, 'box', split_axis=0, concat_axis=3, tiled=True)  29.1 us
    all_to_all x2, starting transfers between devices, shards(): lax.all_to_all(translated, 'box', split_axis=3, concat_axis=0, tiled=True)  27.3 us
    all_to_all x1, starting transfers between devices, shards(): lax.all_to_all(encoded, 'box', split_axis=0, concat_axis=3, tiled=True)  18.6 us
    dot_general x12, matrix products, masked_flips(): jnp.dot(rows, jnp.asarray(matrix, rows.dtype), precision=precision, prefe...  14.1 us
    dot_general x2, matrix products, near_field(): lax.dot_general(pieces.reshape(8, -1, V), blocks, (((2,), (2,)), ((0,), (...  12.8 us
    psum x1, blocking collectives, shards(): first_sum, second_sum = lax.psum((first_sq, second_sq), 'exc')  12.6 us
    dot_general x2, matrix products, translate(): jnp.einsum('kcts,kxes->kcxet', translators, encoded, preferred_element_ty...  6.3 us
    another operation x3, other arithmetic  5.84 us
  transfers between devices with their start and end apart: 7, of which 2 were waited for; matrix products, arithmetic and copies ran while one was open for 30% of the time, Pallas kernels for 0%

profile of v4, /device:TPU:1, one launch (start us, length us, event | category | flops | bytes accessed | tf_op | source)
XLA Modules:
  0.0 182.9 jit_solution(9950493746193436068)
XLA Ops:
  2.1 1.3 convolution_bitcast_fusion.2
  3.4 1.3 convolution_bitcast_fusion.3
  5.9 18.6 %all-to-all-start = ((bf16[512,2,2,4]{3,2,1,0:T(2,128)(2,1)}), bf16[512,2,2,4]{3,2,1,0:T(2,128)(2,1)S(1)}, u32[]{:S(2)}, u32[]{:S(2)}) async-start(bf16[512,2,2,4]{3,2,1,0:T(2,128)(2,1)} %copy.113), calls=%async_computation | async-start | bytes 1048576 | tf_op jit(solution)/shard_map/all_to_all | solution.py:245
  29.5 5.4 %fusion.33 = (f32[512,512]{1,0:T(8,128)S(1)}, f32[512,512]{1,0:T(8,128)S(1)}, f32[512,512]{1,0:T(8,128)S(1)}, f32[512,512]{1,0:T(8,128)S(1)}, f32[512,512]{1,0:T...) fusion(f32[512]{0:T(512)S(1)} %get-tuple-element.51, ...), kind=kLoop, calls=%fused_computation.81 | loop fusion | flops 10747904 | bytes 14686208 | tf_op jit(solution)/shard_map/vmap()/neg | solution.py:54
  34.9 5.8 %multiply_convert_fusion.1 = (bf16[1,4,512,512]{3,2,0,1:T(8,128)(2,1)S(1)}, bf16[1,4,512,512]{3,2,0,1:T(8,128)(2,1)}) fusion(f32[512,512]{1,0:T(8,128)S(1)} %get-tuple-element.42, f32[512,512]{1,0:T(8,128)S(1)} %get-tuple-element.43, f32[512,512]{1,0:T(8,128)S(1)} %get-tuple-element.41, f32[512,512]{1,0:T(8,128)S(1)} %get-tuple-element.36, ...), kind=kLoop, calls=%fused_computation.4 | loop fusion | flops 36700160 | bytes 18874416 | tf_op jit(solution)/shard_map/convert.10
  40.8 1.4 all-to-all-done
  43.2 2.9 %fusion.11 = f32[4,2,2,2,512]{4,3,1,2,0:T(2,128)S(1)} fusion(bf16[1,4,512,512]{3,2,0,1:T(8,128)(2,1)} %get-tuple-element.14, bf16[1,4,512,512]{3,2,0,1:T(8,128)(2,1)S(1)} %get-tuple-element.13, bf16[4,2,2,512,1]{3,2,1,0,4:T(2,128)(2,1)S(1)} %reshape.1316), kind=kOutput, calls=%fused_computation.34 | convolution fusion | flops 25165824 | bytes 4276224 | tf_op jit(solution)/shard_map/kcts,kxes->kcxet/dot_general | solution.py:218
  46.2 2.2 %collective-permute-start = (bf16[2,2,4,512]{3,2,1,0:T(4,128)(2,1)S(1)}, bf16[2,2,4,512]{3,2,1,0:T(4,128)(2,1)S(1)}, u32[]{:S(2)}, u32[]{:S(2)}) collective-permute-start(bf16[2,2,4,512]{3,2,1,0:T(4,128)(2,1)S(1)} %multiply_convert_fusion.3), channel_id=1, source_target_pairs={{0,4},{4,8},{8,12},{12,16},{16,20},{20,24},{24,28},{28,32},{32,36}... | collective-permute-start | bytes 49160 | tf_op jit(solution)/shard_map/ppermute | solution.py:26
  51.1 15.9 %all-to-all-start.1 = ((bf16[4,2,2,512]{0,2,1,3:T(2,128)(2,1)}), bf16[4,2,2,512]{0,2,1,3:T(2,128)(2,1)}, u32[]{:S(2)}, u32[]{:S(2)}) async-start(bf16[4,2,2,512]{0,2,1,3:T(2,128)(2,1)} %copy.123), calls=%async_computation.1 | async-start | bytes 1048576 | tf_op jit(solution)/shard_map/all_to_all | solution.py:249
  67.3 1.3 fusion.10
  68.7 1.3 fusion.9
  70.3 5.9 %fusion.77 = f32[8,32,1024]{2,1,0:T(8,128)S(1)} fusion(bf16[8,32,512]{2,1,0:T(8,128)(2,1)S(1)} %bitcast.219, bf16[8,1024,512]{2,1,0:T(8,128)(2,1)} %constant.138.clone), kind=kOutput, calls=%fused_computation.176 | convolution fusion | flops 268435456 | bytes 9699328 | tf_op jit(solution)/shard_map/dot_general | solution.py:181
  80.6 1.9 %fusion.3 = f32[256,512,1,1]{1,0,3,2:T(8,128)} fusion(f32[256,512]{1,0:T(8,128)S(1)} %convolution_select_fusion.4, f32[512,512]{1,0:T(8,128)S(1)} %copy-done, pred[256]{0:T(512)(128)(4,1)S(1)} %copy-done.7), kind=kOutput, calls=%fused_computation.18 | convolution fusion | flops 805437440 | bytes 2097408 | tf_op jit(solution)/shard_map/dot_general | solution.py:146
  82.4 1.5 all-to-all-done.1
  84.0 2.0 %copy.192 = bf16[4,2,2,128,4]{0,3,4,2,1:T(8,128)(2,1)} copy(bf16[4,2,2,128,4]{0,2,1,4,3:T(2,128)(2,1)} %bitcast.30) | data formatting | bytes 32768 | tf_op jit(solution)/shard_map/all_to_all | solution.py:249
  86.0 1.8 all_to_all.59
  88.5 2.7 %fusion.47 = (f32[4]{0:T(128)S(1)}, bf16[2,2,4,512]{3,2,1,0:T(4,128)(2,1)S(1)}, bf16[2,2,4,512]{3,2,1,0:T(4,128)(2,1)}) fusion(f32[4,512]{1,0:T(4,128)S(1)} %convert_multiply_fusion.2, f32[1,2,4,512]{3,2,1,0:T(4,128)S(1)} %get-tuple-element.28, f32[1,2,4,512]{3,2,1,0:T(4,128)S(1)} %get-tuple-element.27, f32[2,2,4,256]{2,3,1,0:T(8,128)S(1)} %bitcast.207, ...), kind=kOutput, calls=%fused_computation.105 | convolution fusion | flops 25231356 | bytes 614416 | tf_op jit(solution)/shard_map/dot_general | solution.py:201
  92.6 1.3 convolution_bitcast_fusion.1
  94.4 29.1 %all_to_all.72 = bf16[512,2,2,4]{3,2,1,0:T(2,128)(2,1)S(1)} all-to-all(bf16[512,2,2,4]{3,2,1,0:T(2,128)(2,1)S(1)} %copy.126), channel_id=1, replica_groups=mesh['box'=128,'exc'=4] {'box'}, dimensions={0} | all-to-all | bytes 32768 | tf_op jit(solution)/shard_map/all_to_all | solution.py:245
  124.4 3.4 %fusion.12 = f32[4,2,2,2,512]{4,3,1,2,0:T(2,128)S(1)} fusion(bf16[1,4,512,512]{3,2,0,1:T(8,128)(2,1)} %get-tuple-element.14, bf16[1,4,512,512]{3,2,0,1:T(8,128)(2,1)} %copy-done.5, bf16[4,2,2,512,1]{3,2,1,0,4:T(2,128)(2,1)S(1)} %reshape.1321), kind=kOutput, calls=%fused_computation.35 | convolution fusion | flops 25165824 | bytes 4276224 | tf_op jit(solution)/shard_map/kcts,kxes->kcxet/dot_general | solution.py:218
  127.9 2.2 %collective-permute-start.2 = (bf16[2,2,4,512]{3,2,1,0:T(4,128)(2,1)S(1)}, bf16[2,2,4,512]{3,2,1,0:T(4,128)(2,1)S(1)}, u32[]{:S(2)}, u32[]{:S(2)}) collective-permute-start(bf16[2,2,4,512]{3,2,1,0:T(4,128)(2,1)S(1)} %get-tuple-element.9), channel_id=1, source_target_pairs={{0,4},{4,8},{8,12},{12,16},{16,20},{20,24},{24,28},{28,32},{32,36}... | collective-permute-start | bytes 49160 | tf_op jit(solution)/shard_map/ppermute | solution.py:26
  132.6 11.4 %all-to-all-start.3 = ((bf16[4,2,2,512]{0,2,1,3:T(2,128)(2,1)}), bf16[4,2,2,512]{0,2,1,3:T(2,128)(2,1)S(1)}, u32[]{:S(2)}, u32[]{:S(2)}) async-start(bf16[4,2,2,512]{0,2,1,3:T(2,128)(2,1)} %copy.136), calls=%async_computation.3 | async-start | bytes 1048576 | tf_op jit(solution)/shard_map/all_to_all | solution.py:249
  144.3 1.3 fusion.7
  145.6 1.3 fusion.6
  147.0 1.3 fusion.5
  148.3 6.9 %fusion.78 = f32[8,32,1024]{2,1,0:T(8,128)} fusion(bf16[8,32,512]{2,1,0:T(8,128)(2,1)S(1)} %bitcast.218, bf16[8,1024,512]{2,1,0:T(8,128)(2,1)} %constant.138.clone), kind=kOutput, calls=%fused_computation.177 | convolution fusion | flops 268435456 | bytes 9699328 | tf_op jit(solution)/shard_map/dot_general | solution.py:181
  155.3 3.1 %reshape.1312 = f32[8,2,16,2,512]{4,3,2,1,0:T(2,128)} reshape(f32[8,32,1024]{2,1,0:T(8,128)} %fusion.78) | data formatting | bytes 2097152 | tf_op jit(solution)/shard_map/reshape | solution.py:185
  158.3 2.8 %fusion.75 = (f32[8,1,16,1,512]{4,3,2,1,0:T(1,128)S(1)}, f32[8,1,16,1,512]{4,3,2,1,0:T(1,128)S(1)}, f32[8,1,16,1,512]{4,3,2,1,0:T(1,128)S(1)}, f32[8,1,16,1,512]{4,3,2,1,0:T(1,128)S(1)}) fusion(f32[8,2,16,2,512]{4,3,2,1,0:T(2,128)} %reshape.1312), kind=kLoop, calls=%fused_computation.174 | loop fusion | bytes 2097152 | tf_op jit(solution)/shard_map/slice | solution.py:188
  165.4 1.3 fusion.21
  166.7 1.3 fusion.25
  168.0 1.7 multiply_reduce_fusion
  169.7 12.6 %all-reduce = (f32[4]{0:T(128)S(1)}, f32[4]{0:T(128)S(1)}) all-reduce(f32[4]{0:T(128)S(1)} %get-tuple-element.31, f32[4]{0:T(128)S(1)} %get-tuple-element.53), channel_id=1, replica_groups=mesh['box'=128,'exc'=4] {'exc'}, use_global_device_ids=true, to_apply=%region_3.4 | all-reduce | flops 8 | bytes 64 | tf_op jit(solution)/shard_map/psum | solution.py:254
  (91 shorter events, 27.1 us)
Async XLA Ops:
  5.9 36.4 %all-to-all-start = ((bf16[512,2,2,4]{3,2,1,0:T(2,128)(2,1)}), bf16[512,2,2,4]{3,2,1,0:T(2,128)(2,1)S(1)}, u32[]{:S(2)}, u32[]{:S(2)}) async-start(bf16[512,2,2,4]{3,2,1,0:T(2,128)(2,1)} %copy.113), calls=%async_computation | async-start | bytes 1048576 | tf_op jit(solution)/shard_map/all_to_all | solution.py:245
  34.9 5.8 %copy-start.6 = (f32[2,2]{1,0:T(2,128)S(1)}, f32[2,2]{1,0:T(2,128)}, u32[]{:S(2)}) copy-start(f32[2,2]{1,0:T(2,128)} %constant.148) | copy-start | bytes 52
  40.7 10.3 %copy-start.5 = (bf16[1,4,512,512]{3,2,0,1:T(8,128)(2,1)}, bf16[1,4,512,512]{3,2,0,1:T(8,128)(2,1)S(1)}, u32[]{:S(2)}) copy-start(bf16[1,4,512,512]{3,2,0,1:T(8,128)(2,1)S(1)} %get-tuple-element.13) | copy-start | bytes 6291460
  43.2 24.1 %copy-start.9 = (pred[256]{0:T(512)(128)(4,1)S(1)}, pred[256]{0:T(512)(128)(4,1)}, u32[]{:S(2)}) copy-start(pred[256]{0:T(512)(128)(4,1)} %constant.152) | copy-start | bytes 772
  43.2 25.5 %copy-start.8 = (pred[256]{0:T(512)(128)(4,1)S(1)}, pred[256]{0:T(512)(128)(4,1)}, u32[]{:S(2)}) copy-start(pred[256]{0:T(512)(128)(4,1)} %constant.151) | copy-start | bytes 772
  43.2 26.8 %copy-start.7 = (pred[256]{0:T(512)(128)(4,1)S(1)}, pred[256]{0:T(512)(128)(4,1)}, u32[]{:S(2)}) copy-start(pred[256]{0:T(512)(128)(4,1)} %constant.150) | copy-start | bytes 772
  43.2 26.8 %copy-start.10 = (bf16[512,512]{1,0:T(8,128)(2,1)S(1)}, bf16[512,512]{1,0:T(8,128)(2,1)}, u32[]{:S(2)}) copy-start(bf16[512,512]{1,0:T(8,128)(2,1)} %constant.136.clone) | copy-start | bytes 1572868
  46.2 20.8 %collective-permute-start = (bf16[2,2,4,512]{3,2,1,0:T(4,128)(2,1)S(1)}, bf16[2,2,4,512]{3,2,1,0:T(4,128)(2,1)S(1)}, u32[]{:S(2)}, u32[]{:S(2)}) collective-permute-start(bf16[2,2,4,512]{3,2,1,0:T(4,128)(2,1)S(1)} %multiply_convert_fusion.3), channel_id=1, source_target_pairs={{0,4},{4,8},{8,12},{12,16},{16,20},{20,24},{24,28},{28,32},{32,36}... | collective-permute-start | bytes 49160 | tf_op jit(solution)/shard_map/ppermute | solution.py:26
  48.4 18.6 %collective-permute-start.1 = (bf16[2,2,4,512]{3,2,1,0:T(4,128)(2,1)S(1)}, bf16[2,2,4,512]{3,2,1,0:T(4,128)(2,1)S(1)}, u32[]{:S(2)}, u32[]{:S(2)}) collective-permute-start(bf16[2,2,4,512]{3,2,1,0:T(4,128)(2,1)S(1)} %multiply_convert_fusion.3), channel_id=1, source_target_pairs={{4,0},{8,4},{12,8},{16,12},{20,16},{24,20},{28,24},{32,28},{36,32}... | collective-permute-start | bytes 49160 | tf_op jit(solution)/shard_map/ppermute | solution.py:29
  51.1 32.9 %all-to-all-start.1 = ((bf16[4,2,2,512]{0,2,1,3:T(2,128)(2,1)}), bf16[4,2,2,512]{0,2,1,3:T(2,128)(2,1)}, u32[]{:S(2)}, u32[]{:S(2)}) async-start(bf16[4,2,2,512]{0,2,1,3:T(2,128)(2,1)} %copy.123), calls=%async_computation.1 | async-start | bytes 1048576 | tf_op jit(solution)/shard_map/all_to_all | solution.py:249
  76.2 3.3 %copy-start.1 = (f32[512,512]{1,0:T(8,128)S(1)}, f32[512,512]{1,0:T(8,128)}, u32[]{:S(2)}) copy-start(f32[512,512]{1,0:T(8,128)} %constant.140.clone) | copy-start | bytes 3145732
  77.2 1.3 copy-start.2
  77.2 3.4 %copy-start = (f32[512,512]{1,0:T(8,128)S(1)}, f32[512,512]{1,0:T(8,128)}, u32[]{:S(2)}) copy-start(f32[512,512]{1,0:T(8,128)} %constant.141.clone) | copy-start | bytes 3145732
  78.4 9.4 %copy-start.4 = (bf16[2,512,512]{2,1,0:T(8,128)(2,1)S(1)}, bf16[2,512,512]{2,1,0:T(8,128)(2,1)}, u32[]{:S(2)}) copy-start(bf16[2,512,512]{2,1,0:T(8,128)(2,1)} %param.53) | copy-start | bytes 3145732
  127.9 16.1 %collective-permute-start.2 = (bf16[2,2,4,512]{3,2,1,0:T(4,128)(2,1)S(1)}, bf16[2,2,4,512]{3,2,1,0:T(4,128)(2,1)S(1)}, u32[]{:S(2)}, u32[]{:S(2)}) collective-permute-start(bf16[2,2,4,512]{3,2,1,0:T(4,128)(2,1)S(1)} %get-tuple-element.9), channel_id=1, source_target_pairs={{0,4},{4,8},{8,12},{12,16},{16,20},{20,24},{24,28},{28,32},{32,36}... | collective-permute-start | bytes 49160 | tf_op jit(solution)/shard_map/ppermute | solution.py:26
  130.1 13.9 %collective-permute-start.3 = (bf16[2,2,4,512]{3,2,1,0:T(4,128)(2,1)S(1)}, bf16[2,2,4,512]{3,2,1,0:T(4,128)(2,1)S(1)}, u32[]{:S(2)}, u32[]{:S(2)}) collective-permute-start(bf16[2,2,4,512]{3,2,1,0:T(4,128)(2,1)S(1)} %get-tuple-element.9), channel_id=1, source_target_pairs={{4,0},{8,4},{12,8},{16,12},{20,16},{24,20},{28,24},{32,28},{36,32}... | collective-permute-start | bytes 49160 | tf_op jit(solution)/shard_map/ppermute | solution.py:29
  132.6 31.8 %all-to-all-start.3 = ((bf16[4,2,2,512]{0,2,1,3:T(2,128)(2,1)}), bf16[4,2,2,512]{0,2,1,3:T(2,128)(2,1)S(1)}, u32[]{:S(2)}, u32[]{:S(2)}) async-start(bf16[4,2,2,512]{0,2,1,3:T(2,128)(2,1)} %copy.136), calls=%async_computation.3 | async-start | bytes 1048576 | tf_op jit(solution)/shard_map/all_to_all | solution.py:249
  158.3 2.9 %copy-start.3 = (f32[512,512]{1,0:T(8,128)S(1)}, f32[512,512]{1,0:T(8,128)}, u32[]{:S(2)}) copy-start(f32[512,512]{1,0:T(8,128)} %constant.139.clone) | copy-start | bytes 3145732

commit v5 on v4

--- a/solution.py
+++ b/solution.py
@@ -203,14 +203,11 @@
 
 
 def encode(sources, enc_table):
-    real_prod = jnp.einsum(
-        "kv,xebv->kxeb", enc_table[0], sources, preferred_element_type=jnp.float32
-    )
-    imag_prod = jnp.einsum(
-        "kv,xebv->kxeb", enc_table[1], sources, preferred_element_type=jnp.float32
+    product = jnp.einsum(
+        "ckv,xebv->ckxeb", enc_table, sources, preferred_element_type=jnp.float32
     )
     return jnp.stack(
-        [real_prod[:, 0] - imag_prod[:, 1], imag_prod[:, 0] + real_prod[:, 1]], axis=1
+        [product[0, :, 0] - product[1, :, 1], product[1, :, 0] + product[0, :, 1]], axis=1
     ).astype(jnp.bfloat16)
 
 
@@ -224,13 +221,10 @@
 
 
 def decode(returned, dec_table):
-    real_prod = jnp.einsum(
-        "vk,kxeb->xebv", dec_table[0], returned, preferred_element_type=jnp.float32
-    )
-    imag_prod = jnp.einsum(
-        "vk,kxeb->xebv", dec_table[1], returned, preferred_element_type=jnp.float32
-    )
-    return jnp.stack([real_prod[0] - imag_prod[1], imag_prod[0] + real_prod[1]])
+    product = jnp.einsum(
+        "cvk,kxeb->cxebv", dec_table, returned, preferred_element_type=jnp.float32
+    )
+    return jnp.stack([product[0, 0] - product[1, 1], product[1, 0] + product[0, 1]])
 
 
 def shards(incident, contrast, box_pos, directions, enc_table, dec_table):

time: 184 us -> 180 us (0.978)
  matrix products: 46.4 us -> 40.5 us
    dot_general x8 -> x4, matrix products: 8.29 us -> 2.8 us  [the longest x2 2.01 us: decode(): jnp.einsum('cvk,kxeb->cxebv', dec_table, returned, preferred_element_type...]
    another operation x5 -> x3, other arithmetic: 5.88 us -> 6.08 us
where the time goes in v5:
time: 180 us; the launch traced here: 179 us
  starting transfers between devices  53.6 us (30%)
  blocking collectives  40.7 us (23%)
  matrix products  40.5 us (22%)
  local copies, waits for them, and re-layouts  20.9 us (12%)
  other arithmetic  18.2 us (10%)
  waiting for transfers between devices  3.79 us (2%)
    all_to_all x1, blocking collectives, shards(): lax.all_to_all(encoded, 'box', split_axis=0, concat_axis=3, tiled=True)  28.1 us
    all_to_all x2, starting transfers between devices, shards(): lax.all_to_all(translated, 'box', split_axis=3, concat_axis=0, tiled=True)  28 us
    all_to_all x1, starting transfers between devices, shards(): lax.all_to_all(encoded, 'box', split_axis=0, concat_axis=3, tiled=True)  18.6 us
    dot_general x12, matrix products, masked_flips(): jnp.dot(rows, jnp.asarray(matrix, rows.dtype), precision=precision, prefe...  13.1 us
    dot_general x2, matrix products, near_field(): lax.dot_general(pieces.reshape(8, -1, V), blocks, (((2,), (2,)), ((0,), (...  12.8 us
    psum x1, blocking collectives, shards(): first_sum, second_sum = lax.psum((first_sq, second_sq), 'exc')  12.6 us
    dot_general x2, matrix products, translate(): jnp.einsum('kcts,kxes->kcxet', translators, encoded, preferred_element_ty...  6.96 us
    another operation x1, other arithmetic  6.04 us
  transfers between devices with their start and end apart: 7, of which 2 were waited for; matrix products, arithmetic and copies ran while one was open for 30% of the time, Pallas kernels for 0%

profile of v5, /device:TPU:1, one launch (start us, length us, event | category | flops | bytes accessed | tf_op | source)
XLA Modules:
  0.0 179.0 jit_solution(16804795434533385177)
XLA Ops:
  2.6 1.2 copy.133
  3.8 18.6 %all-to-all-start = ((bf16[512,2,2,4]{3,2,1,0:T(2,128)(2,1)}), bf16[512,2,2,4]{3,2,1,0:T(2,128)(2,1)S(1)}, u32[]{:S(2)}, u32[]{:S(2)}) async-start(bf16[512,2,2,4]{3,2,1,0:T(2,128)(2,1)} %copy.133), calls=%async_computation | async-start | bytes 1048576 | tf_op jit(solution)/shard_map/all_to_all | solution.py:239
  27.4 5.4 %fusion.25 = (f32[512,512]{1,0:T(8,128)S(1)}, f32[512,512]{1,0:T(8,128)S(1)}, f32[512,512]{1,0:T(8,128)S(1)}, f32[512,512]{1,0:T(8,128)S(1)}, f32[512,512]{1,0:T...) fusion(f32[512]{0:T(512)S(1)} %get-tuple-element.47, ...), kind=kLoop, calls=%fused_computation.73 | loop fusion | flops 10747904 | bytes 14686208 | tf_op jit(solution)/shard_map/vmap()/neg | solution.py:54
  32.8 6.0 %multiply_convert_fusion.1 = (bf16[1,4,512,512]{3,2,0,1:T(8,128)(2,1)}, bf16[1,4,512,512]{3,2,0,1:T(8,128)(2,1)}) fusion(f32[512,512]{1,0:T(8,128)S(1)} %get-tuple-element.38, f32[512,512]{1,0:T(8,128)S(1)} %get-tuple-element.39, f32[512,512]{1,0:T(8,128)S(1)} %get-tuple-element.37, f32[512,512]{1,0:T(8,128)S(1)} %get-tuple-element.32, ...), kind=kLoop, calls=%fused_computation.4 | loop fusion | flops 36700160 | bytes 18874416 | tf_op jit(solution)/shard_map/convert.12
  38.9 1.2 all-to-all-done
  41.2 3.5 %fusion.11 = f32[4,2,2,2,512]{4,3,1,2,0:T(2,128)S(1)} fusion(bf16[1,4,512,512]{3,2,0,1:T(8,128)(2,1)} %get-tuple-element.14, bf16[1,4,512,512]{3,2,0,1:T(8,128)(2,1)} %get-tuple-element.13, bf16[4,2,2,512,1]{3,2,1,0,4:T(2,128)(2,1)S(1)} %reshape.1464), kind=kOutput, calls=%fused_computation.34 | convolution fusion | flops 25165824 | bytes 4276224 | tf_op jit(solution)/shard_map/kcts,kxes->kcxet/dot_general | solution.py:215
  44.8 2.2 %collective-permute-start = (bf16[2,2,4,512]{3,2,1,0:T(4,128)(2,1)S(1)}, bf16[2,2,4,512]{3,2,1,0:T(4,128)(2,1)S(1)}, u32[]{:S(2)}, u32[]{:S(2)}) collective-permute-start(bf16[2,2,4,512]{3,2,1,0:T(4,128)(2,1)S(1)} %multiply_convert_fusion.3), channel_id=1, source_target_pairs={{0,4},{4,8},{8,12},{12,16},{16,20},{20,24},{24,28},{28,32},{32,36}... | collective-permute-start | bytes 49160 | tf_op jit(solution)/shard_map/ppermute | solution.py:26
  47.0 1.3 collective-permute-start.1
  49.7 16.1 %all-to-all-start.1 = ((bf16[4,2,2,512]{0,2,1,3:T(2,128)(2,1)}), bf16[4,2,2,512]{0,2,1,3:T(2,128)(2,1)}, u32[]{:S(2)}, u32[]{:S(2)}) async-start(bf16[4,2,2,512]{0,2,1,3:T(2,128)(2,1)} %copy.143), calls=%async_computation.1 | async-start | bytes 1048576 | tf_op jit(solution)/shard_map/all_to_all | solution.py:243
  66.1 1.3 fusion.10
  68.1 5.9 %fusion.73 = f32[8,32,1024]{2,1,0:T(8,128)S(1)} fusion(bf16[8,32,512]{2,1,0:T(8,128)(2,1)S(1)} %bitcast.244, bf16[8,1024,512]{2,1,0:T(8,128)(2,1)} %constant.138.clone), kind=kOutput, calls=%fused_computation.174 | convolution fusion | flops 268435456 | bytes 9699328 | tf_op jit(solution)/shard_map/dot_general | solution.py:181
  78.4 1.9 %fusion.3 = f32[256,512,1,1]{1,0,3,2:T(8,128)} fusion(f32[256,512]{1,0:T(8,128)S(1)} %convolution_select_fusion.4, f32[512,512]{1,0:T(8,128)S(1)} %copy-done.1, pred[256]{0:T(512)(128)(4,1)S(1)} %copy-done.8), kind=kOutput, calls=%fused_computation.18 | convolution fusion | flops 805437440 | bytes 2097408 | tf_op jit(solution)/shard_map/dot_general | solution.py:146
  80.2 2.6 %all-to-all-done.1 = bf16[4,2,2,512]{0,2,1,3:T(2,128)(2,1)} async-done(((bf16[4,2,2,512]{0,2,1,3:T(2,128)(2,1)}), bf16[4,2,2,512]{0,2,1,3:T(2,128)(2,1)}, u32[]{:S(2)}, u32[]{:S(2)}) %all-to-all-start.1) | async-done | bytes 16416 | tf_op jit(solution)/shard_map/all_to_all | solution.py:243
  82.8 2.0 %copy.222 = bf16[4,2,2,128,4]{0,3,4,2,1:T(8,128)(2,1)} copy(bf16[4,2,2,128,4]{0,2,1,4,3:T(2,128)(2,1)} %bitcast.29) | data formatting | bytes 32768 | tf_op jit(solution)/shard_map/all_to_all | solution.py:243
  84.8 1.8 %reshape.1467 = bf16[512,2,2,4,1]{0,3,2,1,4:T(4,128)(2,1)S(1)} reshape(bf16[128,4,2,2,4]{1,0,4,3,2:T(8,128)(2,1)} %bitcast.239) | data formatting | bytes 32768 | tf_op jit(solution)/shard_map/all_to_all | solution.py:243
  87.2 2.7 %fusion.31 = (f32[4]{0:T(128)S(1)}, bf16[2,2,4,512]{3,2,1,0:T(4,128)(2,1)S(1)}, bf16[2,2,4,512]{3,2,1,0:T(4,128)(2,1)}) fusion(f32[4,512]{1,0:T(4,128)S(1)} %convert_multiply_fusion.2, f32[1,2,4,512]{3,2,1,0:T(4,128)S(1)} %get-tuple-element.26, f32[1,2,4,512]{3,2,1,0:T(4,128)S(1)} %get-tuple-element.25, f32[2,2,4,256]{2,3,1,0:T(8,128)S(1)} %bitcast.233, ...), kind=kOutput, calls=%fused_computation.89 | convolution fusion | flops 25231356 | bytes 614416 | tf_op jit(solution)/shard_map/dot_general | solution.py:201
  90.9 28.1 %all_to_all.72 = bf16[512,2,2,4]{3,2,1,0:T(2,128)(2,1)S(1)} all-to-all(bf16[512,2,2,4]{3,2,1,0:T(2,128)(2,1)S(1)} %copy.149), channel_id=1, replica_groups=mesh['box'=128,'exc'=4] {'box'}, dimensions={0} | all-to-all | bytes 32768 | tf_op jit(solution)/shard_map/all_to_all | solution.py:239
  119.9 3.4 %fusion.12 = f32[4,2,2,2,512]{4,3,1,2,0:T(2,128)S(1)} fusion(bf16[1,4,512,512]{3,2,0,1:T(8,128)(2,1)} %get-tuple-element.14, bf16[1,4,512,512]{3,2,0,1:T(8,128)(2,1)} %get-tuple-element.13, bf16[4,2,2,512,1]{3,2,1,0,4:T(2,128)(2,1)S(1)} %reshape.1470), kind=kOutput, calls=%fused_computation.35 | convolution fusion | flops 25165824 | bytes 4276224 | tf_op jit(solution)/shard_map/kcts,kxes->kcxet/dot_general | solution.py:215
  123.4 2.2 %collective-permute-start.2 = (bf16[2,2,4,512]{3,2,1,0:T(4,128)(2,1)S(1)}, bf16[2,2,4,512]{3,2,1,0:T(4,128)(2,1)S(1)}, u32[]{:S(2)}, u32[]{:S(2)}) collective-permute-start(bf16[2,2,4,512]{3,2,1,0:T(4,128)(2,1)S(1)} %get-tuple-element.9), channel_id=1, source_target_pairs={{0,4},{4,8},{8,12},{12,16},{16,20},{20,24},{24,28},{28,32},{32,36}... | collective-permute-start | bytes 49160 | tf_op jit(solution)/shard_map/ppermute | solution.py:26
  125.6 1.3 collective-permute-start.3
  126.9 1.2 copy.159
  128.0 11.9 %all-to-all-start.3 = ((bf16[4,2,2,512]{0,2,1,3:T(2,128)(2,1)}), bf16[4,2,2,512]{0,2,1,3:T(2,128)(2,1)}, u32[]{:S(2)}, u32[]{:S(2)}) async-start(bf16[4,2,2,512]{0,2,1,3:T(2,128)(2,1)} %copy.159), calls=%async_computation.3 | async-start | bytes 1048576 | tf_op jit(solution)/shard_map/all_to_all | solution.py:243
  140.3 1.3 fusion.7
  141.6 1.3 fusion.6
  143.0 1.3 fusion.5
  144.3 6.9 %fusion.74 = f32[8,32,1024]{2,1,0:T(8,128)} fusion(bf16[8,32,512]{2,1,0:T(8,128)(2,1)S(1)} %bitcast.243, bf16[8,1024,512]{2,1,0:T(8,128)(2,1)} %constant.138.clone), kind=kOutput, calls=%fused_computation.175 | convolution fusion | flops 268435456 | bytes 9699328 | tf_op jit(solution)/shard_map/dot_general | solution.py:181
  151.3 3.1 %reshape.1460 = f32[8,2,16,2,512]{4,3,2,1,0:T(2,128)} reshape(f32[8,32,1024]{2,1,0:T(8,128)} %fusion.74) | data formatting | bytes 2097152 | tf_op jit(solution)/shard_map/reshape | solution.py:185
  154.3 2.8 %fusion.71 = (f32[8,1,16,1,512]{4,3,2,1,0:T(1,128)S(1)}, f32[8,1,16,1,512]{4,3,2,1,0:T(1,128)S(1)}, f32[8,1,16,1,512]{4,3,2,1,0:T(1,128)S(1)}, f32[8,1,16,1,512]{4,3,2,1,0:T(1,128)S(1)}) fusion(f32[8,2,16,2,512]{4,3,2,1,0:T(2,128)} %reshape.1460), kind=kLoop, calls=%fused_computation.172 | loop fusion | bytes 2097152 | tf_op jit(solution)/shard_map/slice | solution.py:188
  160.5 1.2 copy.220
  162.5 1.6 convolution_bitcast_fusion
  164.1 1.7 multiply_reduce_fusion
  165.8 12.6 %all-reduce = (f32[4]{0:T(128)S(1)}, f32[4]{0:T(128)S(1)}) all-reduce(f32[4]{0:T(128)S(1)} %get-tuple-element.27, f32[4]{0:T(128)S(1)} %get-tuple-element.49), channel_id=1, replica_groups=mesh['box'=128,'exc'=4] {'exc'}, use_global_device_ids=true, to_apply=%region_3.4 | all-reduce | flops 8 | bytes 64 | tf_op jit(solution)/shard_map/psum | solution.py:248
  (93 shorter events, 21.9 us)
Async XLA Ops:
  0.6 1.5 copy-start
  3.8 36.4 %all-to-all-start = ((bf16[512,2,2,4]{3,2,1,0:T(2,128)(2,1)}), bf16[512,2,2,4]{3,2,1,0:T(2,128)(2,1)S(1)}, u32[]{:S(2)}, u32[]{:S(2)}) async-start(bf16[512,2,2,4]{3,2,1,0:T(2,128)(2,1)} %copy.133), calls=%async_computation | async-start | bytes 1048576 | tf_op jit(solution)/shard_map/all_to_all | solution.py:239
  32.8 6.1 %copy-start.7 = (f32[2,2]{1,0:T(2,128)S(1)}, f32[2,2]{1,0:T(2,128)}, u32[]{:S(2)}) copy-start(f32[2,2]{1,0:T(2,128)} %constant.148) | copy-start | bytes 52
  41.1 25.0 %copy-start.10 = (pred[256]{0:T(512)(128)(4,1)S(1)}, pred[256]{0:T(512)(128)(4,1)}, u32[]{:S(2)}) copy-start(pred[256]{0:T(512)(128)(4,1)} %constant.152) | copy-start | bytes 772
  41.1 26.3 %copy-start.9 = (pred[256]{0:T(512)(128)(4,1)S(1)}, pred[256]{0:T(512)(128)(4,1)}, u32[]{:S(2)}) copy-start(pred[256]{0:T(512)(128)(4,1)} %constant.151) | copy-start | bytes 772
  41.1 26.3 %copy-start.12 = (bf16[512,512]{1,0:T(8,128)(2,1)S(1)}, bf16[512,512]{1,0:T(8,128)(2,1)}, u32[]{:S(2)}) copy-start(bf16[512,512]{1,0:T(8,128)(2,1)} %constant.134.clone) | copy-start | bytes 1572868
  41.1 26.6 %copy-start.8 = (pred[256]{0:T(512)(128)(4,1)S(1)}, pred[256]{0:T(512)(128)(4,1)}, u32[]{:S(2)}) copy-start(pred[256]{0:T(512)(128)(4,1)} %constant.150) | copy-start | bytes 772
  41.1 26.6 %copy-start.11 = (bf16[512,512]{1,0:T(8,128)(2,1)S(1)}, bf16[512,512]{1,0:T(8,128)(2,1)}, u32[]{:S(2)}) copy-start(bf16[512,512]{1,0:T(8,128)(2,1)} %constant.136.clone) | copy-start | bytes 1572868
  44.8 21.0 %collective-permute-start = (bf16[2,2,4,512]{3,2,1,0:T(4,128)(2,1)S(1)}, bf16[2,2,4,512]{3,2,1,0:T(4,128)(2,1)S(1)}, u32[]{:S(2)}, u32[]{:S(2)}) collective-permute-start(bf16[2,2,4,512]{3,2,1,0:T(4,128)(2,1)S(1)} %multiply_convert_fusion.3), channel_id=1, source_target_pairs={{0,4},{4,8},{8,12},{12,16},{16,20},{20,24},{24,28},{28,32},{32,36}... | collective-permute-start | bytes 49160 | tf_op jit(solution)/shard_map/ppermute | solution.py:26
  47.0 18.8 %collective-permute-start.1 = (bf16[2,2,4,512]{3,2,1,0:T(4,128)(2,1)S(1)}, bf16[2,2,4,512]{3,2,1,0:T(4,128)(2,1)S(1)}, u32[]{:S(2)}, u32[]{:S(2)}) collective-permute-start(bf16[2,2,4,512]{3,2,1,0:T(4,128)(2,1)S(1)} %multiply_convert_fusion.3), channel_id=1, source_target_pairs={{4,0},{8,4},{12,8},{16,12},{20,16},{24,20},{28,24},{32,28},{36,32}... | collective-permute-start | bytes 49160 | tf_op jit(solution)/shard_map/ppermute | solution.py:29
  49.7 33.1 %all-to-all-start.1 = ((bf16[4,2,2,512]{0,2,1,3:T(2,128)(2,1)}), bf16[4,2,2,512]{0,2,1,3:T(2,128)(2,1)}, u32[]{:S(2)}, u32[]{:S(2)}) async-start(bf16[4,2,2,512]{0,2,1,3:T(2,128)(2,1)} %copy.143), calls=%async_computation.1 | async-start | bytes 1048576 | tf_op jit(solution)/shard_map/all_to_all | solution.py:243
  74.9 1.3 copy-start.4
  74.9 2.4 %copy-start.2 = (f32[512,512]{1,0:T(8,128)S(1)}, f32[512,512]{1,0:T(8,128)}, u32[]{:S(2)}) copy-start(f32[512,512]{1,0:T(8,128)} %constant.140.clone) | copy-start | bytes 3145732
  74.9 3.4 %copy-start.1 = (f32[512,512]{1,0:T(8,128)S(1)}, f32[512,512]{1,0:T(8,128)}, u32[]{:S(2)}) copy-start(f32[512,512]{1,0:T(8,128)} %constant.141.clone) | copy-start | bytes 3145732
  76.2 10.4 %copy-start.6 = (bf16[2,512,512]{2,1,0:T(8,128)(2,1)S(1)}, bf16[2,512,512]{2,1,0:T(8,128)(2,1)}, u32[]{:S(2)}) copy-start(bf16[2,512,512]{2,1,0:T(8,128)(2,1)} %param.53) | copy-start | bytes 3145732
  123.4 16.6 %collective-permute-start.2 = (bf16[2,2,4,512]{3,2,1,0:T(4,128)(2,1)S(1)}, bf16[2,2,4,512]{3,2,1,0:T(4,128)(2,1)S(1)}, u32[]{:S(2)}, u32[]{:S(2)}) collective-permute-start(bf16[2,2,4,512]{3,2,1,0:T(4,128)(2,1)S(1)} %get-tuple-element.9), channel_id=1, source_target_pairs={{0,4},{4,8},{8,12},{12,16},{16,20},{20,24},{24,28},{28,32},{32,36}... | collective-permute-start | bytes 49160 | tf_op jit(solution)/shard_map/ppermute | solution.py:26
  125.6 14.4 %collective-permute-start.3 = (bf16[2,2,4,512]{3,2,1,0:T(4,128)(2,1)S(1)}, bf16[2,2,4,512]{3,2,1,0:T(4,128)(2,1)S(1)}, u32[]{:S(2)}, u32[]{:S(2)}) collective-permute-start(bf16[2,2,4,512]{3,2,1,0:T(4,128)(2,1)S(1)} %get-tuple-element.9), channel_id=1, source_target_pairs={{4,0},{8,4},{12,8},{16,12},{20,16},{24,20},{28,24},{32,28},{36,32}... | collective-permute-start | bytes 49160 | tf_op jit(solution)/shard_map/ppermute | solution.py:29
  128.0 32.5 %all-to-all-start.3 = ((bf16[4,2,2,512]{0,2,1,3:T(2,128)(2,1)}), bf16[4,2,2,512]{0,2,1,3:T(2,128)(2,1)}, u32[]{:S(2)}, u32[]{:S(2)}) async-start(bf16[4,2,2,512]{0,2,1,3:T(2,128)(2,1)} %copy.159), calls=%async_computation.3 | async-start | bytes 1048576 | tf_op jit(solution)/shard_map/all_to_all | solution.py:243
  154.3 3.0 %copy-start.5 = (f32[512,512]{1,0:T(8,128)S(1)}, f32[512,512]{1,0:T(8,128)}, u32[]{:S(2)}) copy-start(f32[512,512]{1,0:T(8,128)} %constant.139.clone) | copy-start | bytes 3145732
  154.3 4.0 %copy-start.3 = (f32[512,512]{1,0:T(8,128)S(1)}, f32[512,512]{1,0:T(8,128)}, u32[]{:S(2)}) copy-start(f32[512,512]{1,0:T(8,128)} %constant.140.clone) | copy-start | bytes 3145732
